TPU v7x, 256 devices: a whole 4x4x8 slice. The times are simulated.
256 devices in a mesh: wave: 8 (over z_lo, core), tile: 32 (over x, z_hi, y).
Axes of the slice: x: 4, y: 4, z: 8 (z_hi: 2, z_lo: 4; z = z_hi * 4 + z_lo), core: 2. Of those that a mesh axis runs over, the one named last changes fastest.
Arguments:
- thickness: float32 [32, 256, 256], P('tile'), may hold values from 0 to 1
- illumination: float32 [16, 2, 256, 256], P('wave'), may hold values from -6 to 6
- absorb: float32 [16], P('wave'), may hold values from 0.1 to 0.8
- phases: float32 [16], P('wave'), may hold values from 0.1 to 0.8
- amplitudes: bfloat16 [32, 6, 16, 256, 256], P('tile', None, 'wave'), may hold values from 0.049804688 to 0.5
- positions: int32 [32, 6, 2], P('tile'), may hold values from 0 to 255, as said below
- batch_order: int32 [32, 6], P('tile'), may hold values from 0 to 5, each once within a row
- live_slots: int32 [32, 3, 2], P('tile'), may hold values from 0 to 1, as said below
Outputs:
- thickness_new: float32 [32, 256, 256], P('tile')
Inputs may be any that keep to these rules, and one draw needn't show every extreme that they name: `positions`: offsets inside the tile that owns the pattern; the 256 x 256 window from every slot's corner lies inside the object. `live_slots`: in every batch at least one tile has its slot 0 live.
All inputs are finite; a program needn't handle non-finite values.
Results may differ from a plain program's by a relative error of at most 0.0003.
Values sent between devices are 32-bit elements; how exact they have to be, the bound alone decides.
No kernel may reach another device: no remote copies, remote signals or barrier semaphores. Data moves between devices by JAX's collectives and lax.ppermute only.
A program may use at most 64 MiB of HBM per device.

v0:
```python
import math

import jax
import jax.numpy as jnp
from jax import lax
from jax.sharding import PartitionSpec as P

GRID_X = 8
BATCHES = 3


def passed_along(block, axis, distance):
    devices = range(lax.axis_size(axis))
    route = [(i - distance, i) for i in devices if i - distance in devices]
    return lax.ppermute(block, axis, route)


def tables(points):
    counter = jnp.arange(points, dtype=jnp.int32)
    angles = (
        2.0 * math.pi / points * (counter[:, None] * counter[None, :] % points).astype(jnp.float32)
    )
    factor = 1.0 / math.sqrt(points)
    return (
        (jnp.cos(angles) * factor).astype(jnp.bfloat16),
        (-jnp.sin(angles) * factor).astype(jnp.bfloat16),
    )


def left_apply(real_part, imag_part, left_real, left_imag):
    points = real_part.shape[0]
    stacked = jnp.concatenate([real_part, imag_part], 0)
    joined = jnp.concatenate([left_real, left_imag], -1)
    product = jnp.einsum("ij,...jk->...ik", stacked, joined, preferred_element_type=jnp.float32)
    return (
        product[..., :points, :points] - product[..., points:, points:],
        product[..., :points, points:] + product[..., points:, :points],
    )


def right_apply(real_part, imag_part, left_real, left_imag):
    points = real_part.shape[0]
    stacked = jnp.concatenate([real_part, imag_part], 1)
    joined = jnp.concatenate([left_real, left_imag], -2)
    product = jnp.einsum("...ij,jk->...ik", joined, stacked, preferred_element_type=jnp.float32)
    return (
        product[..., :points, :points] - product[..., points:, points:],
        product[..., :points, points:] + product[..., points:, :points],
    )


def window_terms(cells, illumination, absorb, phases, measured, alive, cos_table, sin_table):
    absorb_col = absorb[None, :, None, None]
    phase_col = phases[None, :, None, None]
    spread = cells[:, None, :, :]
    magnitude = jnp.exp(-absorb_col * spread)
    object_real = magnitude * jnp.cos(phase_col * spread)
    object_imag = magnitude * jnp.sin(phase_col * spread)
    probe_real = illumination[None, :, 0]
    probe_imag = illumination[None, :, 1]
    wave_real = probe_real * object_real - probe_imag * object_imag
    wave_imag = probe_real * object_imag + probe_imag * object_real
    half_real, half_imag = left_apply(
        cos_table, sin_table, wave_real.astype(jnp.bfloat16), wave_imag.astype(jnp.bfloat16)
    )
    far_real, far_imag = right_apply(
        cos_table, sin_table, half_real.astype(jnp.bfloat16), half_imag.astype(jnp.bfloat16)
    )
    modulus = jnp.sqrt(far_real * far_real + far_imag * far_imag + 0.25)
    ratio = measured.astype(jnp.float32) / modulus
    fixed_real = (far_real * ratio).astype(jnp.bfloat16)
    fixed_imag = (far_imag * ratio).astype(jnp.bfloat16)
    back_real, back_imag = left_apply(cos_table, -sin_table, fixed_real, fixed_imag)
    new_real, new_imag = right_apply(
        cos_table, -sin_table, back_real.astype(jnp.bfloat16), back_imag.astype(jnp.bfloat16)
    )
    slope_real = -absorb_col * wave_real - phase_col * wave_imag
    slope_imag = -absorb_col * wave_imag + phase_col * wave_real
    change_real = new_real - wave_real
    change_imag = new_imag - wave_imag
    weight_live = alive.astype(jnp.float32)[:, None, None]
    numerator = jnp.sum(slope_real * change_real + slope_imag * change_imag, axis=1) * weight_live
    weights = jnp.sum(slope_real * slope_real + slope_imag * slope_imag, axis=1) * weight_live
    return (numerator, weights)


def move_rims(strips, offset):
    return passed_along(strips, "tile", offset)


def shards(thickness, illumination, absorb, phases, amplitudes, positions, batch_order, live_slots):
    tile_now = thickness[0]
    tile_height, tile_width = tile_now.shape
    window = illumination.shape[-1]
    slots = live_slots.shape[2]
    column = lax.axis_index("tile") % GRID_X
    keep_right = (column != GRID_X - 1).astype(jnp.float32)
    keep_left = (column != 0).astype(jnp.float32)
    cos_table, sin_table = tables(window)
    for batch_index in range(BATCHES):
        strip_right = move_rims(tile_now[None, :, :window], -1)[0] * keep_right
        widened = jnp.concatenate([tile_now, strip_right], 1)
        strip_below = move_rims(widened[None, :window, :], -GRID_X)[0]
        extended = jnp.concatenate([widened, strip_below], 0)
        chosen = batch_order[0, batch_index * slots : (batch_index + 1) * slots]
        places = positions[0][chosen]
        measured = amplitudes[0][chosen]
        alive = live_slots[0, batch_index]
        cells = jax.vmap(
            lambda place: lax.dynamic_slice(extended, (place[0], place[1]), (window, window))
        )(places)
        numer_win, weight_win = window_terms(
            cells, illumination, absorb, phases, measured, alive, cos_table, sin_table
        )
        numer_win, weight_win = lax.psum((numer_win, weight_win), "wave")

        def add_window(slot_index, totals):
            numer_map, weight_map = totals
            row_at = places[slot_index, 0]
            col_at = places[slot_index, 1]
            numer_map = lax.dynamic_update_slice(
                numer_map,
                lax.dynamic_slice(numer_map, (row_at, col_at), (window, window))
                + numer_win[slot_index],
                (row_at, col_at),
            )
            weight_map = lax.dynamic_update_slice(
                weight_map,
                lax.dynamic_slice(weight_map, (row_at, col_at), (window, window))
                + weight_win[slot_index],
                (row_at, col_at),
            )
            return (numer_map, weight_map)

        empty = jnp.zeros((tile_height + window, tile_width + window), jnp.float32)
        numer_map, weight_map = lax.fori_loop(0, slots, add_window, (empty, empty))
        stacked = jnp.stack([numer_map, weight_map])
        arrived_below = move_rims(stacked[:, tile_height:, :], GRID_X)
        folded = stacked[:, :tile_height, :].at[:, :window, :].add(arrived_below)
        arrived_side = move_rims(folded[:, :, tile_width:], 1) * keep_left
        maps = folded[:, :, :tile_width].at[:, :, :window].add(arrived_side)
        largest = lax.pmax(jnp.max(maps[1]), "tile")
        tile_now = tile_now + 0.5 * maps[0] / (0.75 * maps[1] + 0.25 * largest)
    return tile_now[None]


def solution(mesh):
    placed = (
        P("tile", None, None),
        P("wave", None, None, None),
        P("wave"),
        P("wave"),
        P("tile", None, "wave", None, None),
        P("tile", None, None),
        P("tile", None),
        P("tile", None, None),
    )
    return jax.shard_map(
        shards, mesh=mesh, in_specs=placed, out_specs=P("tile", None, None), check_vma=False
    )
```

profile of v0, /device:TPU:1, one launch (start us, length us, event | category | flops | bytes accessed | tf_op | source)
XLA Modules:
  0.0 953.1 jit_solution(16841867864628957839)
XLA Ops:
  24.1 21.2 %collective-permute-done.1 = f32[1,256,512]{2,1,0:T(8,128)} collective-permute-done((f32[1,256,512]{2,1,0:T(8,128)}, f32[1,256,512]{2,1,0:T(8,128)}, u32[]{:S(2)}, u32[]{:S(2)}) %collective-permute-start.1) | collective-permute-done | bytes 524320 | tf_op jit(solution)/shard_map/ppermute | solution.py:15
  47.5 7.5 while.63
  55.1 4.5 fusion.128
  63.8 5.1 add_reduce_fusion.2
  70.1 76.5 %all-reduce.11.cloned.1.call-done = (f32[2,256,256]{2,1,0:T(8,128)}, f32[2,256,256]{2,1,0:T(8,128)}) async-done(((f32[2,256,256]{2,1,0:T(8,128)}, f32[2,256,256]{2,1,0:T(8,128)}), (f32[2,256,256]{2,1,0:T(8,128)}, f32[2,256,256]{2,1,0:T(8,128)})) %all-reduce.11.cloned.1.call-update) | async-done | bytes 1048592 | tf_op jit(solution)/shard_map/psum | solution.py:115
  148.9 25.2 %while.60 = (s32[]{:T(128)}, f32[512,512]{1,0:T(8,128)}, f32[512,512]{1,0:T(8,128)}, s32[2,2]{1,0:T(2,128)S(1)}, f32[2,256,256]{2,1,0:T(8,128)}, /*index=5*/f32[...) while((s32[]{:T(128)}, f32[512,512]{1,0:T(8,128)}, f32[512,512]{1,0:T(8,128)}, s32[2,2]{1,0:T(2,128)S(1)}, ...), condition=%wide.region_5.6_spmd, body=%wide.region_4.5_spmd.sunk | while | flops 131080 | bytes 2621641 | solution.py:136
  179.2 19.6 %collective-permute-done.2 = f32[2,256,512]{2,1,0:T(8,128)S(1)} collective-permute-done((f32[2,256,512]{2,1,0:T(8,128)S(1)}, f32[2,256,512]{2,1,0:T(8,128)S(1)}, u32[]{:S(2)}, u32[]{:S(2)}) %collective-permute-start.2) | collective-permute-done | bytes 1048608 | tf_op jit(solution)/shard_map/ppermute | solution.py:15
  200.1 4.7 collective-permute-start.3
  204.7 6.8 collective-permute-done.3
  213.4 107.8 %pmax.21 = f32[]{:T(128)} all-reduce(f32[]{:T(128)} %slice_reduce_fusion.2), channel_id=1, replica_groups=mesh['wave'=8,'tile'=32] {'tile'}, use_global_device_ids=true, to_apply=%region_7.8 | all-reduce | flops 1 | bytes 8 | tf_op jit(solution)/shard_map/pmax | solution.py:142
  326.6 4.4 collective-permute-done.4
  345.4 7.3 while.64
  352.8 4.5 fusion.130
  361.5 5.1 add_reduce_fusion.1
  367.8 92.2 %all-reduce.9.cloned.1.call-done = (f32[2,256,256]{2,1,0:T(8,128)}, f32[2,256,256]{2,1,0:T(8,128)}) async-done(((f32[2,256,256]{2,1,0:T(8,128)}, f32[2,256,256]{2,1,0:T(8,128)}), (f32[2,256,256]{2,1,0:T(8,128)}, f32[2,256,256]{2,1,0:T(8,128)})) %all-reduce.9.cloned.1.call-update) | async-done | bytes 1048592 | tf_op jit(solution)/shard_map/psum | solution.py:115
  462.3 26.3 %while.61 = (s32[]{:T(128)}, f32[512,512]{1,0:T(8,128)}, f32[512,512]{1,0:T(8,128)}, s32[2,2]{1,0:T(2,128)S(1)}, f32[2,256,256]{2,1,0:T(8,128)}, /*index=5*/f32[...) while((s32[]{:T(128)}, f32[512,512]{1,0:T(8,128)}, f32[512,512]{1,0:T(8,128)}, s32[2,2]{1,0:T(2,128)S(1)}, ...), condition=%wide.region_13.14_spmd, body=%wide.region_12.13_spmd.sunk | while | flops 131080 | bytes 2621641 | solution.py:136
  490.0 4.0 collective-permute-start.6
  494.0 19.6 %collective-permute-done.6 = f32[2,256,512]{2,1,0:T(8,128)S(1)} collective-permute-done((f32[2,256,512]{2,1,0:T(8,128)S(1)}, f32[2,256,512]{2,1,0:T(8,128)S(1)}, u32[]{:S(2)}, u32[]{:S(2)}) %collective-permute-start.6) | collective-permute-done | bytes 1048608 | tf_op jit(solution)/shard_map/ppermute | solution.py:15
  517.1 7.5 collective-permute-done.7
  525.5 107.1 %pmax.22 = f32[]{:T(128)} all-reduce(f32[]{:T(128)} %slice_reduce_fusion.1), channel_id=1, replica_groups=mesh['wave'=8,'tile'=32] {'tile'}, use_global_device_ids=true, to_apply=%region_15.16 | all-reduce | flops 1 | bytes 8 | tf_op jit(solution)/shard_map/pmax | solution.py:142
  638.0 4.5 collective-permute-done.8
  656.9 7.0 while.65
  663.9 4.5 fusion.132
  672.7 5.1 add_reduce_fusion
  678.9 92.8 %all-reduce.7.cloned.1.call-done = (f32[2,256,256]{2,1,0:T(8,128)}, f32[2,256,256]{2,1,0:T(8,128)}) async-done(((f32[2,256,256]{2,1,0:T(8,128)}, f32[2,256,256]{2,1,0:T(8,128)}), (f32[2,256,256]{2,1,0:T(8,128)}, f32[2,256,256]{2,1,0:T(8,128)})) %all-reduce.7.cloned.1.call-update) | async-done | bytes 1048592 | tf_op jit(solution)/shard_map/psum | solution.py:115
  772.9 27.7 %while.62 = (s32[]{:T(128)}, f32[512,512]{1,0:T(8,128)S(1)}, f32[512,512]{1,0:T(8,128)}, s32[2,2]{1,0:T(2,128)S(1)}, f32[2,256,256]{2,1,0:T(8,128)}, /*index=5*/...) while((s32[]{:T(128)}, f32[512,512]{1,0:T(8,128)S(1)}, f32[512,512]{1,0:T(8,128)}, ...), condition=%wide.region_21.22_spmd, body=%wide.region_20.21_spmd.sunk | while | flops 131080 | bytes 2621641 | solution.py:136
  782.2 4.1 dynamic_update_slice.52
  795.8 4.9 dynamic_update_slice.52
  803.3 19.8 %collective-permute-done.10 = f32[2,256,512]{2,1,0:T(8,128)S(1)} collective-permute-done((f32[2,256,512]{2,1,0:T(8,128)S(1)}, f32[2,256,512]{2,1,0:T(8,128)S(1)}, u32[]{:S(2)}, u32[]{:S(2)}) %collective-permute-start.10) | collective-permute-done | bytes 1048608 | tf_op jit(solution)/shard_map/ppermute | solution.py:15
  823.3 4.4 collective-permute-start.11
  827.7 7.5 collective-permute-done.11
  836.0 108.1 %pmax.23 = f32[]{:T(128)} all-reduce(f32[]{:T(128)} %slice_reduce_fusion), channel_id=1, replica_groups=mesh['wave'=8,'tile'=32] {'tile'}, use_global_device_ids=true, to_apply=%region_23.24 | all-reduce | flops 1 | bytes 8 | tf_op jit(solution)/shard_map/pmax | solution.py:142
  (197 shorter events, 168.9 us)
Async XLA Ops:
  6.5 12.6 %copy-start = (bf16[1,6,2,256,256]{4,3,2,1,0:T(8,128)(2,1)S(1)}, bf16[1,6,2,256,256]{4,3,2,1,0:T(8,128)(2,1)}, u32[]{:S(2)}) copy-start(bf16[1,6,2,256,256]{4,3,2,1,0:T(8,128)(2,1)} %param.42) | copy-start | bytes 4718596
  6.5 140.1 %all-reduce.11.cloned.1.call-start = ((), (), s32[]{:S(2)}) async-start(), calls=%async_computation.2 | async-start | bytes 2097152 | tf_op jit(solution)/shard_map/psum | solution.py:115
  6.5 8.1 collective-permute-start
  16.5 28.8 %collective-permute-start.1 = (f32[1,256,512]{2,1,0:T(8,128)}, f32[1,256,512]{2,1,0:T(8,128)}, u32[]{:S(2)}, u32[]{:S(2)}) collective-permute-start(f32[1,256,512]{2,1,0:T(8,128)} %maximum_bitcast_fusion), channel_id=1, source_target_pairs={{8,0},{9,1},{10,2},{11,3},{12,4},{13,5},{14,6},{15,7},{16,8},{17,9... | collective-permute-start | bytes 1572872 | tf_op jit(solution)/shard_map/ppermute | solution.py:15
  19.1 26.2 %copy-start.7 = (f32[1,256,256]{2,1,0:T(8,128)S(1)}, f32[1,256,256]{2,1,0:T(8,128)}, u32[]{:S(2)}) copy-start(f32[1,256,256]{2,1,0:T(8,128)} %param.38) | copy-start | bytes 786436
  47.5 7.6 copy-start.15
  63.8 5.1 copy-start.18
  70.1 390.0 %all-reduce.9.cloned.1.call-start = ((), (), s32[]{:S(2)}) async-start(), calls=%async_computation.1 | async-start | bytes 2097152 | tf_op jit(solution)/shard_map/psum | solution.py:115
  174.1 24.7 %copy-start.2 = (f32[512,512]{1,0:T(8,128)S(1)}, f32[512,512]{1,0:T(8,128)}, u32[]{:S(2)}) copy-start(f32[512,512]{1,0:T(8,128)} %get-tuple-element.455) | copy-start | bytes 3145732
  174.1 24.7 %copy-start.3 = (f32[512,512]{1,0:T(8,128)S(1)}, f32[512,512]{1,0:T(8,128)}, u32[]{:S(2)}) copy-start(f32[512,512]{1,0:T(8,128)} %get-tuple-element.456) | copy-start | bytes 3145732
  175.5 23.3 %collective-permute-start.2 = (f32[2,256,512]{2,1,0:T(8,128)S(1)}, f32[2,256,512]{2,1,0:T(8,128)S(1)}, u32[]{:S(2)}, u32[]{:S(2)}) collective-permute-start(f32[2,256,512]{2,1,0:T(8,128)S(1)} %pad_maximum_fusion.2), channel_id=1, source_target_pairs={{0,8},{1,9},{2,10},{3,11},{4,12},{5,13},{6,14},{7,15},{8,16},{9,17... | collective-permute-start | bytes 3145736 | tf_op jit(solution)/shard_map/ppermute | solution.py:15
  200.0 124.9 %copy-start.20 = (s32[2,1]{0,1:T(1,128)S(1)}, s32[2,1]{0,1:T(1,128)}, u32[]{:S(2)}) copy-start(s32[2,1]{0,1:T(1,128)} %get-tuple-element.614) | copy-start | bytes 28
  200.1 11.4 %collective-permute-start.3 = (f32[2,256,256]{2,1,0:T(8,128)S(1)}, f32[2,256,256]{2,1,0:T(8,128)}, u32[]{:S(2)}, u32[]{:S(2)}) collective-permute-start(f32[2,256,256]{2,1,0:T(8,128)S(1)} %slice.505), channel_id=1, source_target_pairs={{0,1},{1,2},{2,3},{3,4},{4,5},{5,6},{6,7},{7,8},{8,9},{9,10},{10,1... | collective-permute-start | bytes 1572872 | tf_op jit(solution)/shard_map/ppermute | solution.py:15
  323.6 7.4 collective-permute-start.4
  325.6 8.9 copy-start.22
  326.6 5.4 copy-start.8
  332.9 10.4 %copy-start.9 = (f32[256,256]{1,0:T(8,128)S(1)}, f32[256,256]{1,0:T(8,128)}, u32[]{:S(2)}) copy-start(f32[256,256]{1,0:T(8,128)} %copy-done.8) | copy-start | bytes 786436
  332.9 10.4 %collective-permute-start.5 = (f32[1,256,512]{2,1,0:T(8,128)}, f32[1,256,512]{2,1,0:T(8,128)}, u32[]{:S(2)}, u32[]{:S(2)}) collective-permute-start(f32[1,256,512]{2,1,0:T(8,128)} %maximum_bitcast_fusion.1), channel_id=1, source_target_pairs={{8,0},{9,1},{10,2},{11,3},{12,4},{13,5},{14,6},{15,7},{16,8},{17,9... | collective-permute-start | bytes 1572872 | tf_op jit(solution)/shard_map/ppermute | solution.py:15
  367.8 403.9 %all-reduce.7.cloned.1.call-start = ((), (), s32[]{:S(2)}) async-start(), calls=%async_computation | async-start | bytes 2097152 | tf_op jit(solution)/shard_map/psum | solution.py:115
  488.6 25.0 %copy-start.4 = (f32[512,512]{1,0:T(8,128)S(1)}, f32[512,512]{1,0:T(8,128)}, u32[]{:S(2)}) copy-start(f32[512,512]{1,0:T(8,128)} %get-tuple-element.457) | copy-start | bytes 3145732
  488.6 25.0 %copy-start.5 = (f32[512,512]{1,0:T(8,128)S(1)}, f32[512,512]{1,0:T(8,128)}, u32[]{:S(2)}) copy-start(f32[512,512]{1,0:T(8,128)} %get-tuple-element.458) | copy-start | bytes 3145732
  490.0 23.6 %collective-permute-start.6 = (f32[2,256,512]{2,1,0:T(8,128)S(1)}, f32[2,256,512]{2,1,0:T(8,128)S(1)}, u32[]{:S(2)}, u32[]{:S(2)}) collective-permute-start(f32[2,256,512]{2,1,0:T(8,128)S(1)} %pad_maximum_fusion.1), channel_id=1, source_target_pairs={{0,8},{1,9},{2,10},{3,11},{4,12},{5,13},{6,14},{7,15},{8,16},{9,17... | collective-permute-start | bytes 3145736 | tf_op jit(solution)/shard_map/ppermute | solution.py:15
  513.8 122.5 %copy-start.19 = (s32[2,1]{0,1:T(1,128)S(1)}, s32[2,1]{0,1:T(1,128)}, u32[]{:S(2)}) copy-start(s32[2,1]{0,1:T(1,128)} %get-tuple-element.612) | copy-start | bytes 28
  513.8 10.8 %collective-permute-start.7 = (f32[2,256,256]{2,1,0:T(8,128)S(1)}, f32[2,256,256]{2,1,0:T(8,128)S(1)}, u32[]{:S(2)}, u32[]{:S(2)}) collective-permute-start(f32[2,256,256]{2,1,0:T(8,128)S(1)} %slice.527), channel_id=1, source_target_pairs={{0,1},{1,2},{2,3},{3,4},{4,5},{5,6},{6,7},{7,8},{8,9},{9,10},{10,1... | collective-permute-start | bytes 1572872 | tf_op jit(solution)/shard_map/ppermute | solution.py:15
  635.0 7.4 collective-permute-start.8
  637.0 9.0 copy-start.21
  638.0 5.5 copy-start.10
  644.3 10.4 %copy-start.11 = (f32[256,256]{1,0:T(8,128)S(1)}, f32[256,256]{1,0:T(8,128)}, u32[]{:S(2)}) copy-start(f32[256,256]{1,0:T(8,128)} %copy-done.10) | copy-start | bytes 786436
  644.3 10.4 %collective-permute-start.9 = (f32[1,256,512]{2,1,0:T(8,128)}, f32[1,256,512]{2,1,0:T(8,128)}, u32[]{:S(2)}, u32[]{:S(2)}) collective-permute-start(f32[1,256,512]{2,1,0:T(8,128)} %maximum_bitcast_fusion.2), channel_id=1, source_target_pairs={{8,0},{9,1},{10,2},{11,3},{12,4},{13,5},{14,6},{15,7},{16,8},{17,9... | collective-permute-start | bytes 1572872 | tf_op jit(solution)/shard_map/ppermute | solution.py:15
  800.7 22.3 %copy-start.1 = (f32[512,512]{1,0:T(8,128)S(1)}, f32[512,512]{1,0:T(8,128)}, u32[]{:S(2)}) copy-start(f32[512,512]{1,0:T(8,128)} %get-tuple-element.460) | copy-start | bytes 3145732
  801.9 21.1 %collective-permute-start.10 = (f32[2,256,512]{2,1,0:T(8,128)S(1)}, f32[2,256,512]{2,1,0:T(8,128)S(1)}, u32[]{:S(2)}, u32[]{:S(2)}) collective-permute-start(f32[2,256,512]{2,1,0:T(8,128)S(1)} %pad_maximum_fusion), channel_id=1, source_target_pairs={{0,8},{1,9},{2,10},{3,11},{4,12},{5,13},{6,14},{7,15},{8,16},{9,17... | collective-permute-start | bytes 3145736 | tf_op jit(solution)/shard_map/ppermute | solution.py:15
  823.3 11.9 %collective-permute-start.11 = (f32[2,256,256]{2,1,0:T(8,128)S(1)}, f32[2,256,256]{2,1,0:T(8,128)S(1)}, u32[]{:S(2)}, u32[]{:S(2)}) collective-permute-start(f32[2,256,256]{2,1,0:T(8,128)S(1)} %slice.549), channel_id=1, source_target_pairs={{0,1},{1,2},{2,3},{3,4},{4,5},{5,6},{6,7},{7,8},{8,9},{9,10},{10,1... | collective-permute-start | bytes 1572872 | tf_op jit(solution)/shard_map/ppermute | solution.py:15
  (6 other events, 14.3 us)
Sparse Core Ops, SparseCore 0:
  70.2 76.4 all-reduce.10
  367.9 92.1 all-reduce.8
  679.0 92.5 all-reduce.6
where the time goes:
time: 972 us; the launch traced here: 953 us
  waiting for transfers between devices  381 us (39%)
  blocking collectives  323 us (33%)
  local copies, waits for them, and re-layouts  93.2 us (10%)
  other arithmetic  79.3 us (8%)
  starting transfers between devices  29.9 us (3%)
  loops' own time  22.4 us (2%)
  between operations  15.7 us (2%)
    pmax x3, blocking collectives, shards(): largest = lax.pmax(jnp.max(maps[1]), 'tile')  323 us
    psum x3, waiting for transfers between devices, shards(): numer_win, weight_win = lax.psum((numer_win, weight_win), 'wave')  262 us
    ppermute x12, waiting for transfers between devices, passed_along(): return lax.ppermute(block, axis, route)  119 us
    ppermute x12, starting transfers between devices, passed_along(): return lax.ppermute(block, axis, route)  29.8 us
    dynamic_update_slice x6, local copies, waits for them, and re-layouts, add_window(): lax.dynamic_update_slice(numer_map, lax.dynamic_slice(numer_map, (row_at,...  23 us
    another operation x3, loops' own time, shards(): numer_map, weight_map = lax.fori_loop(0, slots, add_window, (empty, empty))  22.2 us
    gather x18, local copies, waits for them, and re-layouts  21.8 us
    dynamic_update_slice x6, local copies, waits for them, and re-layouts, add_window(): lax.dynamic_update_slice(weight_map, lax.dynamic_slice(weight_map, (row_a...  21.5 us
  transfers between devices with their start and end apart: 15, of which 15 were waited for; matrix products, arithmetic and copies ran while one was open for 3% of the time, Pallas kernels for 0%

commit v1 on v0

--- a/solution.py
+++ b/solution.py
@@ -84,6 +84,13 @@
     return (numerator, weights)
 
 
+def tile_max(value):
+    count = lax.axis_size("tile")
+    spread = jnp.broadcast_to(value, (count, 128))
+    gathered = lax.all_to_all(spread, "tile", 0, 0, tiled=True)
+    return jnp.max(gathered)
+
+
 def move_rims(strips, offset):
     return passed_along(strips, "tile", offset)
 
@@ -139,7 +146,7 @@
         folded = stacked[:, :tile_height, :].at[:, :window, :].add(arrived_below)
         arrived_side = move_rims(folded[:, :, tile_width:], 1) * keep_left
         maps = folded[:, :, :tile_width].at[:, :, :window].add(arrived_side)
-        largest = lax.pmax(jnp.max(maps[1]), "tile")
+        largest = tile_max(jnp.max(maps[1]))
         tile_now = tile_now + 0.5 * maps[0] / (0.75 * maps[1] + 0.25 * largest)
     return tile_now[None]
 

time: 972 us -> 744 us (0.77)
  blocking collectives: 323 us -> 98.5 us
    pmax x3 -> x0, blocking collectives: 323 us -> none  [shards(): largest = lax.pmax(jnp.max(maps[1]), 'tile')]
    all_to_all x0 -> x3, blocking collectives: none -> 98.5 us  [tile_max(): gathered = lax.all_to_all(spread, 'tile', 0, 0, tiled=True)]
where the time goes in v1:
time: 744 us; the launch traced here: 731 us
  waiting for transfers between devices  378 us (51%)
  blocking collectives  98.5 us (13%)
  local copies, waits for them, and re-layouts  94.1 us (13%)
  other arithmetic  82.7 us (11%)
  starting transfers between devices  30.8 us (4%)
  loops' own time  22.4 us (3%)
  between operations  15.7 us (2%)
  matrix products  8.8 us (1%)
    psum x3, waiting for transfers between devices, shards(): numer_win, weight_win = lax.psum((numer_win, weight_win), 'wave')  258 us
    ppermute x12, waiting for transfers between devices, passed_along(): return lax.ppermute(block, axis, route)  119 us
    all_to_all x3, blocking collectives, tile_max(): gathered = lax.all_to_all(spread, 'tile', 0, 0, tiled=True)  98.5 us
    ppermute x12, starting transfers between devices, passed_along(): return lax.ppermute(block, axis, route)  30.8 us
    another operation x3, loops' own time, shards(): numer_map, weight_map = lax.fori_loop(0, slots, add_window, (empty, empty))  22.2 us
    gather x18, local copies, waits for them, and re-layouts  21.8 us
    dynamic_update_slice x6, local copies, waits for them, and re-layouts, add_window(): lax.dynamic_update_slice(weight_map, lax.dynamic_slice(weight_map, (row_a...  21.7 us
    dynamic_update_slice x6, local copies, waits for them, and re-layouts, add_window(): lax.dynamic_update_slice(numer_map, lax.dynamic_slice(numer_map, (row_at,...  21.6 us
  transfers between devices with their start and end apart: 15, of which 15 were waited for; matrix products, arithmetic and copies ran while one was open for 3% of the time, Pallas kernels for 0%

profile of v1, /device:TPU:1, one launch (start us, length us, event | category | flops | bytes accessed | tf_op | source)
XLA Modules:
  0.0 730.6 jit_solution(11967711167071945583)
XLA Ops:
  24.1 21.2 %collective-permute-done.1 = f32[1,256,512]{2,1,0:T(8,128)} collective-permute-done((f32[1,256,512]{2,1,0:T(8,128)}, f32[1,256,512]{2,1,0:T(8,128)}, u32[]{:S(2)}, u32[]{:S(2)}) %collective-permute-start.1) | collective-permute-done | bytes 524320 | tf_op jit(solution)/shard_map/ppermute | solution.py:15
  47.5 7.5 %while.63 = (s32[]{:T(128)}, f32[512,512]{1,0:T(8,128)}, s32[2,2]{1,0:T(2,128)}, f32[2,256,256]{2,1,0:T(8,128)S(1)}, s32[]{:T(128)}) while((s32[]{:T(128)}, f32[512,512]{1,0:T(8,128)}, s32[2,2]{1,0:T(2,128)}, f32[2,256,256]{2,1,0:T(8,128)S(1)}, s32[]{:T(128)}) %tuple.203), condition=%wide.while_cond.6, body=%wide.while_body.6.sunk | while | flops 2 | bytes 524397 | solution.py:117
  55.1 4.5 fusion.128
  63.8 5.1 add_reduce_fusion.2
  70.1 76.5 %all-reduce.11.cloned.1.call-done = (f32[2,256,256]{2,1,0:T(8,128)}, f32[2,256,256]{2,1,0:T(8,128)}) async-done(((f32[2,256,256]{2,1,0:T(8,128)}, f32[2,256,256]{2,1,0:T(8,128)}), (f32[2,256,256]{2,1,0:T(8,128)}, f32[2,256,256]{2,1,0:T(8,128)})) %all-reduce.11.cloned.1.call-update) | async-done | bytes 1048592 | tf_op jit(solution)/shard_map/psum | solution.py:122
  148.9 26.1 %while.60 = (s32[]{:T(128)}, f32[512,512]{1,0:T(8,128)}, f32[512,512]{1,0:T(8,128)}, s32[2,2]{1,0:T(2,128)S(1)}, f32[2,256,256]{2,1,0:T(8,128)}, /*index=5*/f32[...) while((s32[]{:T(128)}, f32[512,512]{1,0:T(8,128)}, f32[512,512]{1,0:T(8,128)}, s32[2,2]{1,0:T(2,128)S(1)}, ...), condition=%wide.region_5.6_spmd, body=%wide.region_4.5_spmd.sunk | while | flops 131080 | bytes 2621641 | solution.py:143
  176.4 4.1 collective-permute-start.2
  180.4 19.6 %collective-permute-done.2 = f32[2,256,512]{2,1,0:T(8,128)S(1)} collective-permute-done((f32[2,256,512]{2,1,0:T(8,128)S(1)}, f32[2,256,512]{2,1,0:T(8,128)S(1)}, u32[]{:S(2)}, u32[]{:S(2)}) %collective-permute-start.2) | collective-permute-done | bytes 1048608 | tf_op jit(solution)/shard_map/ppermute | solution.py:15
  201.3 3.8 collective-permute-start.3
  205.1 6.8 collective-permute-done.3
  214.4 32.1 %all_to_all.18 = f32[32,1,128]{2,1,0:T(1,128)} all-to-all(f32[32,1,128]{2,1,0:T(1,128)S(1)} %broadcast_in_dim.13), channel_id=1, replica_groups=mesh['wave'=8,'tile'=32] {'tile'}, dimensions={0} | all-to-all | bytes 32768 | tf_op jit(solution)/shard_map/all_to_all | solution.py:90
  253.2 4.4 collective-permute-done.4
  272.3 7.3 %while.64 = (s32[]{:T(128)}, f32[512,512]{1,0:T(8,128)}, s32[2,2]{1,0:T(2,128)}, f32[2,256,256]{2,1,0:T(8,128)S(1)}, s32[]{:T(128)}) while((s32[]{:T(128)}, f32[512,512]{1,0:T(8,128)}, s32[2,2]{1,0:T(2,128)}, f32[2,256,256]{2,1,0:T(8,128)S(1)}, s32[]{:T(128)}) %tuple.209), condition=%wide.while_cond.7, body=%wide.while_body.7.sunk | while | flops 2 | bytes 524397 | solution.py:117
  279.6 4.5 fusion.130
  288.3 5.1 add_reduce_fusion.1
  294.7 91.6 %all-reduce.9.cloned.1.call-done = (f32[2,256,256]{2,1,0:T(8,128)}, f32[2,256,256]{2,1,0:T(8,128)}) async-done(((f32[2,256,256]{2,1,0:T(8,128)}, f32[2,256,256]{2,1,0:T(8,128)}), (f32[2,256,256]{2,1,0:T(8,128)}, f32[2,256,256]{2,1,0:T(8,128)})) %all-reduce.9.cloned.1.call-update) | async-done | bytes 1048592 | tf_op jit(solution)/shard_map/psum | solution.py:122
  388.5 26.9 %while.61 = (s32[]{:T(128)}, f32[512,512]{1,0:T(8,128)}, f32[512,512]{1,0:T(8,128)}, s32[2,2]{1,0:T(2,128)S(1)}, f32[2,256,256]{2,1,0:T(8,128)}, /*index=5*/f32[...) while((s32[]{:T(128)}, f32[512,512]{1,0:T(8,128)}, f32[512,512]{1,0:T(8,128)}, s32[2,2]{1,0:T(2,128)S(1)}, ...), condition=%wide.region_13.14_spmd, body=%wide.region_12.13_spmd.sunk | while | flops 131080 | bytes 2621641 | solution.py:143
  394.5 3.8 dynamic_update_slice.51
  398.4 3.8 dynamic_update_slice.50
  420.0 19.6 %collective-permute-done.6 = f32[2,256,512]{2,1,0:T(8,128)S(1)} collective-permute-done((f32[2,256,512]{2,1,0:T(8,128)S(1)}, f32[2,256,512]{2,1,0:T(8,128)S(1)}, u32[]{:S(2)}, u32[]{:S(2)}) %collective-permute-start.6) | collective-permute-done | bytes 1048608 | tf_op jit(solution)/shard_map/ppermute | solution.py:15
  443.2 7.5 %collective-permute-done.7 = f32[2,256,256]{2,1,0:T(8,128)S(1)} collective-permute-done((f32[2,256,256]{2,1,0:T(8,128)S(1)}, f32[2,256,256]{2,1,0:T(8,128)S(1)}, u32[]{:S(2)}, u32[]{:S(2)}) %collective-permute-start.7) | collective-permute-done | bytes 524320 | tf_op jit(solution)/shard_map/ppermute | solution.py:15
  452.3 33.0 %all_to_all.19 = f32[32,1,128]{2,1,0:T(1,128)} all-to-all(f32[32,1,128]{2,1,0:T(1,128)S(1)} %broadcast_in_dim.15), channel_id=1, replica_groups=mesh['wave'=8,'tile'=32] {'tile'}, dimensions={0} | all-to-all | bytes 32768 | tf_op jit(solution)/shard_map/all_to_all | solution.py:90
  492.0 4.5 collective-permute-done.8
  510.9 7.0 while.65
  517.9 4.5 fusion.132
  526.7 5.1 add_reduce_fusion
  532.9 90.1 %all-reduce.7.cloned.1.call-done = (f32[2,256,256]{2,1,0:T(8,128)}, f32[2,256,256]{2,1,0:T(8,128)}) async-done(((f32[2,256,256]{2,1,0:T(8,128)}, f32[2,256,256]{2,1,0:T(8,128)}), (f32[2,256,256]{2,1,0:T(8,128)}, f32[2,256,256]{2,1,0:T(8,128)})) %all-reduce.7.cloned.1.call-update) | async-done | bytes 1048592 | tf_op jit(solution)/shard_map/psum | solution.py:122
  624.3 25.2 %while.62 = (s32[]{:T(128)}, f32[512,512]{1,0:T(8,128)S(1)}, f32[512,512]{1,0:T(8,128)}, s32[2,2]{1,0:T(2,128)S(1)}, f32[2,256,256]{2,1,0:T(8,128)}, /*index=5*/...) while((s32[]{:T(128)}, f32[512,512]{1,0:T(8,128)S(1)}, f32[512,512]{1,0:T(8,128)}, ...), condition=%wide.region_21.22_spmd, body=%wide.region_20.21_spmd.sunk | while | flops 131080 | bytes 2621641 | solution.py:143
  650.6 4.2 collective-permute-start.10
  654.8 19.6 %collective-permute-done.10 = f32[2,256,512]{2,1,0:T(8,128)S(1)} collective-permute-done((f32[2,256,512]{2,1,0:T(8,128)S(1)}, f32[2,256,512]{2,1,0:T(8,128)S(1)}, u32[]{:S(2)}, u32[]{:S(2)}) %collective-permute-start.10) | collective-permute-done | bytes 1048608 | tf_op jit(solution)/shard_map/ppermute | solution.py:15
  678.4 7.8 %collective-permute-done.11 = f32[2,256,256]{2,1,0:T(8,128)S(1)} collective-permute-done((f32[2,256,256]{2,1,0:T(8,128)S(1)}, f32[2,256,256]{2,1,0:T(8,128)S(1)}, u32[]{:S(2)}, u32[]{:S(2)}) %collective-permute-start.11) | collective-permute-done | bytes 524320 | tf_op jit(solution)/shard_map/ppermute | solution.py:15
  687.7 33.4 %all_to_all.20 = f32[32,1,128]{2,1,0:T(1,128)S(1)} all-to-all(f32[32,1,128]{2,1,0:T(1,128)S(1)} %broadcast_in_dim.17), channel_id=1, replica_groups=mesh['wave'=8,'tile'=32] {'tile'}, dimensions={0} | all-to-all | bytes 32768 | tf_op jit(solution)/shard_map/all_to_all | solution.py:90
  (203 shorter events, 176.7 us)
Async XLA Ops:
  6.5 12.6 %copy-start = (bf16[1,6,2,256,256]{4,3,2,1,0:T(8,128)(2,1)S(1)}, bf16[1,6,2,256,256]{4,3,2,1,0:T(8,128)(2,1)}, u32[]{:S(2)}) copy-start(bf16[1,6,2,256,256]{4,3,2,1,0:T(8,128)(2,1)} %param.42) | copy-start | bytes 4718596
  6.5 140.1 %all-reduce.11.cloned.1.call-start = ((), (), s32[]{:S(2)}) async-start(), calls=%async_computation.5 | async-start | bytes 2097152 | tf_op jit(solution)/shard_map/psum | solution.py:122
  6.5 8.1 %collective-permute-start = (f32[1,256,256]{2,1,0:T(8,128)}, f32[1,256,256]{2,1,0:T(8,128)S(1)}, u32[]{:S(2)}, u32[]{:S(2)}) collective-permute-start(f32[1,256,256]{2,1,0:T(8,128)} %param.38), channel_id=1, source_target_pairs={{1,0},{2,1},{3,2},{4,3},{5,4},{6,5},{7,6},{8,7},{9,8},{10,9},{11,1... | collective-permute-start | bytes 786440 | tf_op jit(solution)/shard_map/ppermute | solution.py:15
  16.5 28.8 %collective-permute-start.1 = (f32[1,256,512]{2,1,0:T(8,128)}, f32[1,256,512]{2,1,0:T(8,128)}, u32[]{:S(2)}, u32[]{:S(2)}) collective-permute-start(f32[1,256,512]{2,1,0:T(8,128)} %maximum_bitcast_fusion), channel_id=1, source_target_pairs={{8,0},{9,1},{10,2},{11,3},{12,4},{13,5},{14,6},{15,7},{16,8},{17,9... | collective-permute-start | bytes 1572872 | tf_op jit(solution)/shard_map/ppermute | solution.py:15
  19.1 26.2 %copy-start.7 = (f32[1,256,256]{2,1,0:T(8,128)S(1)}, f32[1,256,256]{2,1,0:T(8,128)}, u32[]{:S(2)}) copy-start(f32[1,256,256]{2,1,0:T(8,128)} %param.38) | copy-start | bytes 786436
  47.5 7.6 %copy-start.15 = (f32[2]{0:T(128)S(1)}, f32[2]{0:T(128)}, u32[]{:S(2)}) copy-start(f32[2]{0:T(128)} %param.41) | copy-start | bytes 28
  63.8 5.1 copy-start.18
  70.1 316.2 %all-reduce.9.cloned.1.call-start = ((), (), s32[]{:S(2)}) async-start(), calls=%async_computation.4 | async-start | bytes 2097152 | tf_op jit(solution)/shard_map/psum | solution.py:122
  174.9 25.1 %copy-start.2 = (f32[512,512]{1,0:T(8,128)S(1)}, f32[512,512]{1,0:T(8,128)}, u32[]{:S(2)}) copy-start(f32[512,512]{1,0:T(8,128)} %get-tuple-element.455) | copy-start | bytes 3145732
  174.9 25.1 %copy-start.3 = (f32[512,512]{1,0:T(8,128)S(1)}, f32[512,512]{1,0:T(8,128)}, u32[]{:S(2)}) copy-start(f32[512,512]{1,0:T(8,128)} %get-tuple-element.456) | copy-start | bytes 3145732
  176.4 23.7 %collective-permute-start.2 = (f32[2,256,512]{2,1,0:T(8,128)S(1)}, f32[2,256,512]{2,1,0:T(8,128)S(1)}, u32[]{:S(2)}, u32[]{:S(2)}) collective-permute-start(f32[2,256,512]{2,1,0:T(8,128)S(1)} %pad_maximum_fusion.2), channel_id=1, source_target_pairs={{0,8},{1,9},{2,10},{3,11},{4,12},{5,13},{6,14},{7,15},{8,16},{9,17... | collective-permute-start | bytes 3145736 | tf_op jit(solution)/shard_map/ppermute | solution.py:15
  201.3 50.3 %copy-start.20 = (s32[2,1]{0,1:T(1,128)S(1)}, s32[2,1]{0,1:T(1,128)}, u32[]{:S(2)}) copy-start(s32[2,1]{0,1:T(1,128)} %get-tuple-element.614) | copy-start | bytes 28
  201.3 10.5 %collective-permute-start.3 = (f32[2,256,256]{2,1,0:T(8,128)S(1)}, f32[2,256,256]{2,1,0:T(8,128)}, u32[]{:S(2)}, u32[]{:S(2)}) collective-permute-start(f32[2,256,256]{2,1,0:T(8,128)S(1)} %slice.505), channel_id=1, source_target_pairs={{0,1},{1,2},{2,3},{3,4},{4,5},{5,6},{6,7},{7,8},{8,9},{9,10},{10,1... | collective-permute-start | bytes 1572872 | tf_op jit(solution)/shard_map/ppermute | solution.py:15
  250.2 7.4 %collective-permute-start.4 = (f32[1,256,256]{2,1,0:T(8,128)}, f32[1,256,256]{2,1,0:T(8,128)}, u32[]{:S(2)}, u32[]{:S(2)}) collective-permute-start(f32[1,256,256]{2,1,0:T(8,128)} %fusion.126), channel_id=1, source_target_pairs={{1,0},{2,1},{3,2},{4,3},{5,4},{6,5},{7,6},{8,7},{9,8},{10,9},{11,1... | collective-permute-start | bytes 786440 | tf_op jit(solution)/shard_map/ppermute | solution.py:15
  252.2 8.9 %copy-start.22 = (s32[2,1]{1,0:T(2,128)S(1)}, s32[2,1]{1,0:T(2,128)}, u32[]{:S(2)}) copy-start(s32[2,1]{1,0:T(2,128)} %copy.77) | copy-start | bytes 28
  253.2 5.4 copy-start.8
  259.5 10.5 %copy-start.9 = (f32[256,256]{1,0:T(8,128)S(1)}, f32[256,256]{1,0:T(8,128)}, u32[]{:S(2)}) copy-start(f32[256,256]{1,0:T(8,128)} %copy-done.8) | copy-start | bytes 786436
  259.5 10.5 %collective-permute-start.5 = (f32[1,256,512]{2,1,0:T(8,128)}, f32[1,256,512]{2,1,0:T(8,128)}, u32[]{:S(2)}, u32[]{:S(2)}) collective-permute-start(f32[1,256,512]{2,1,0:T(8,128)} %maximum_bitcast_fusion.1), channel_id=1, source_target_pairs={{8,0},{9,1},{10,2},{11,3},{12,4},{13,5},{14,6},{15,7},{16,8},{17,9... | collective-permute-start | bytes 1572872 | tf_op jit(solution)/shard_map/ppermute | solution.py:15
  294.6 328.4 %all-reduce.7.cloned.1.call-start = ((), (), s32[]{:S(2)}) async-start(), calls=%async_computation.3 | async-start | bytes 2097152 | tf_op jit(solution)/shard_map/psum | solution.py:122
  415.3 24.2 %copy-start.4 = (f32[512,512]{1,0:T(8,128)S(1)}, f32[512,512]{1,0:T(8,128)}, u32[]{:S(2)}) copy-start(f32[512,512]{1,0:T(8,128)} %get-tuple-element.457) | copy-start | bytes 3145732
  415.3 24.2 %copy-start.5 = (f32[512,512]{1,0:T(8,128)S(1)}, f32[512,512]{1,0:T(8,128)}, u32[]{:S(2)}) copy-start(f32[512,512]{1,0:T(8,128)} %get-tuple-element.458) | copy-start | bytes 3145732
  416.8 22.8 %collective-permute-start.6 = (f32[2,256,512]{2,1,0:T(8,128)S(1)}, f32[2,256,512]{2,1,0:T(8,128)S(1)}, u32[]{:S(2)}, u32[]{:S(2)}) collective-permute-start(f32[2,256,512]{2,1,0:T(8,128)S(1)} %pad_maximum_fusion.1), channel_id=1, source_target_pairs={{0,8},{1,9},{2,10},{3,11},{4,12},{5,13},{6,14},{7,15},{8,16},{9,17... | collective-permute-start | bytes 3145736 | tf_op jit(solution)/shard_map/ppermute | solution.py:15
  439.8 50.5 %copy-start.19 = (s32[2,1]{0,1:T(1,128)S(1)}, s32[2,1]{0,1:T(1,128)}, u32[]{:S(2)}) copy-start(s32[2,1]{0,1:T(1,128)} %get-tuple-element.612) | copy-start | bytes 28
  439.9 10.9 %collective-permute-start.7 = (f32[2,256,256]{2,1,0:T(8,128)S(1)}, f32[2,256,256]{2,1,0:T(8,128)S(1)}, u32[]{:S(2)}, u32[]{:S(2)}) collective-permute-start(f32[2,256,256]{2,1,0:T(8,128)S(1)} %slice.527), channel_id=1, source_target_pairs={{0,1},{1,2},{2,3},{3,4},{4,5},{5,6},{6,7},{7,8},{8,9},{9,10},{10,1... | collective-permute-start | bytes 1572872 | tf_op jit(solution)/shard_map/ppermute | solution.py:15
  489.0 7.4 %collective-permute-start.8 = (f32[1,256,256]{2,1,0:T(8,128)}, f32[1,256,256]{2,1,0:T(8,128)}, u32[]{:S(2)}, u32[]{:S(2)}) collective-permute-start(f32[1,256,256]{2,1,0:T(8,128)} %fusion.127), channel_id=1, source_target_pairs={{1,0},{2,1},{3,2},{4,3},{5,4},{6,5},{7,6},{8,7},{9,8},{10,9},{11,1... | collective-permute-start | bytes 786440 | tf_op jit(solution)/shard_map/ppermute | solution.py:15
  491.0 9.0 %copy-start.21 = (s32[2,1]{1,0:T(2,128)S(1)}, s32[2,1]{1,0:T(2,128)}, u32[]{:S(2)}) copy-start(s32[2,1]{1,0:T(2,128)} %copy.85) | copy-start | bytes 28
  492.0 5.5 copy-start.10
  498.3 10.4 %copy-start.11 = (f32[256,256]{1,0:T(8,128)S(1)}, f32[256,256]{1,0:T(8,128)}, u32[]{:S(2)}) copy-start(f32[256,256]{1,0:T(8,128)} %copy-done.10) | copy-start | bytes 786436
  498.3 10.4 %collective-permute-start.9 = (f32[1,256,512]{2,1,0:T(8,128)}, f32[1,256,512]{2,1,0:T(8,128)}, u32[]{:S(2)}, u32[]{:S(2)}) collective-permute-start(f32[1,256,512]{2,1,0:T(8,128)} %maximum_bitcast_fusion.2), channel_id=1, source_target_pairs={{8,0},{9,1},{10,2},{11,3},{12,4},{13,5},{14,6},{15,7},{16,8},{17,9... | collective-permute-start | bytes 1572872 | tf_op jit(solution)/shard_map/ppermute | solution.py:15
  649.4 25.0 %copy-start.1 = (f32[512,512]{1,0:T(8,128)S(1)}, f32[512,512]{1,0:T(8,128)}, u32[]{:S(2)}) copy-start(f32[512,512]{1,0:T(8,128)} %get-tuple-element.460) | copy-start | bytes 3145732
  650.6 23.8 %collective-permute-start.10 = (f32[2,256,512]{2,1,0:T(8,128)S(1)}, f32[2,256,512]{2,1,0:T(8,128)S(1)}, u32[]{:S(2)}, u32[]{:S(2)}) collective-permute-start(f32[2,256,512]{2,1,0:T(8,128)S(1)} %pad_maximum_fusion), channel_id=1, source_target_pairs={{0,8},{1,9},{2,10},{3,11},{4,12},{5,13},{6,14},{7,15},{8,16},{9,17... | collective-permute-start | bytes 3145736 | tf_op jit(solution)/shard_map/ppermute | solution.py:15
  674.7 11.5 %collective-permute-start.11 = (f32[2,256,256]{2,1,0:T(8,128)S(1)}, f32[2,256,256]{2,1,0:T(8,128)S(1)}, u32[]{:S(2)}, u32[]{:S(2)}) collective-permute-start(f32[2,256,256]{2,1,0:T(8,128)S(1)} %slice.549), channel_id=1, source_target_pairs={{0,1},{1,2},{2,3},{3,4},{4,5},{5,6},{6,7},{7,8},{8,9},{9,10},{10,1... | collective-permute-start | bytes 1572872 | tf_op jit(solution)/shard_map/ppermute | solution.py:15
  (6 other events, 14.3 us)
Sparse Core Ops, SparseCore 0:
  70.2 76.4 all-reduce.10
  294.7 91.4 all-reduce.8
  533.1 89.8 all-reduce.6

commit v2 on v1

--- a/solution.py
+++ b/solution.py
@@ -7,12 +7,6 @@
 
 GRID_X = 8
 BATCHES = 3
-
-
-def passed_along(block, axis, distance):
-    devices = range(lax.axis_size(axis))
-    route = [(i - distance, i) for i in devices if i - distance in devices]
-    return lax.ppermute(block, axis, route)
 
 
 def tables(points):
@@ -91,8 +85,37 @@
     return jnp.max(gathered)
 
 
-def move_rims(strips, offset):
-    return passed_along(strips, "tile", offset)
+def from_offset(block, axis, distance):
+    devices = range(lax.axis_size(axis))
+    route = [(i + distance, i) for i in devices if i + distance in devices]
+    return lax.ppermute(block, axis, route)
+
+
+def partner(block, bit):
+    return lax.ppermute(block, "wave", [(i, i ^ bit) for i in range(lax.axis_size("wave"))])
+
+
+def wave_sum(maps):
+    count = lax.axis_size("wave")
+    rows = maps.shape[1] // 2
+    odd = lax.axis_index("wave") % 2
+    kept = lax.dynamic_slice_in_dim(maps, odd * rows, rows, axis=1)
+    given = lax.dynamic_slice_in_dim(maps, (1 - odd) * rows, rows, axis=1)
+    half = kept + partner(given, 1)
+    bit = 2
+    while bit < count:
+        half = half + partner(half, bit)
+        bit *= 2
+    other = partner(half, 1)
+    low = jnp.where(odd == 0, half, other)
+    high = jnp.where(odd == 0, other, half)
+    return jnp.concatenate([low, high], 1)
+
+
+def picker(offsets, size, span):
+    cells = lax.broadcasted_iota(jnp.int32, (offsets.shape[0], size, span), 1)
+    spots = lax.broadcasted_iota(jnp.int32, (offsets.shape[0], size, span), 2)
+    return (cells == spots + offsets[:, None, None]).astype(jnp.float32)
 
 
 def shards(thickness, illumination, absorb, phases, amplitudes, positions, batch_order, live_slots):
@@ -104,48 +127,35 @@
     keep_right = (column != GRID_X - 1).astype(jnp.float32)
     keep_left = (column != 0).astype(jnp.float32)
     cos_table, sin_table = tables(window)
+    exact = lax.Precision.HIGHEST
     for batch_index in range(BATCHES):
-        strip_right = move_rims(tile_now[None, :, :window], -1)[0] * keep_right
-        widened = jnp.concatenate([tile_now, strip_right], 1)
-        strip_below = move_rims(widened[None, :window, :], -GRID_X)[0]
-        extended = jnp.concatenate([widened, strip_below], 0)
+        right = from_offset(tile_now, "tile", 1) * keep_right
+        below = from_offset(tile_now, "tile", GRID_X)
+        corner = from_offset(tile_now, "tile", GRID_X + 1) * keep_right
+        extended = jnp.concatenate(
+            [jnp.concatenate([tile_now, right], 1), jnp.concatenate([below, corner], 1)], 0
+        )
         chosen = batch_order[0, batch_index * slots : (batch_index + 1) * slots]
         places = positions[0][chosen]
         measured = amplitudes[0][chosen]
         alive = live_slots[0, batch_index]
-        cells = jax.vmap(
-            lambda place: lax.dynamic_slice(extended, (place[0], place[1]), (window, window))
-        )(places)
+        row_pick = picker(places[:, 0], tile_height + window, window)
+        col_pick = picker(places[:, 1], tile_width + window, window)
+        strips = jnp.einsum("sij,ik->sjk", row_pick, extended, precision=exact)
+        cells = jnp.einsum("sjk,skl->sjl", strips, col_pick, precision=exact)
         numer_win, weight_win = window_terms(
             cells, illumination, absorb, phases, measured, alive, cos_table, sin_table
         )
-        numer_win, weight_win = lax.psum((numer_win, weight_win), "wave")
-
-        def add_window(slot_index, totals):
-            numer_map, weight_map = totals
-            row_at = places[slot_index, 0]
-            col_at = places[slot_index, 1]
-            numer_map = lax.dynamic_update_slice(
-                numer_map,
-                lax.dynamic_slice(numer_map, (row_at, col_at), (window, window))
-                + numer_win[slot_index],
-                (row_at, col_at),
-            )
-            weight_map = lax.dynamic_update_slice(
-                weight_map,
-                lax.dynamic_slice(weight_map, (row_at, col_at), (window, window))
-                + weight_win[slot_index],
-                (row_at, col_at),
-            )
-            return (numer_map, weight_map)
-
-        empty = jnp.zeros((tile_height + window, tile_width + window), jnp.float32)
-        numer_map, weight_map = lax.fori_loop(0, slots, add_window, (empty, empty))
-        stacked = jnp.stack([numer_map, weight_map])
-        arrived_below = move_rims(stacked[:, tile_height:, :], GRID_X)
-        folded = stacked[:, :tile_height, :].at[:, :window, :].add(arrived_below)
-        arrived_side = move_rims(folded[:, :, tile_width:], 1) * keep_left
-        maps = folded[:, :, :tile_width].at[:, :, :window].add(arrived_side)
+        wins = jnp.stack([numer_win, weight_win], 1)
+        placed_rows = jnp.einsum("sij,smjk->smik", row_pick, wins, precision=exact)
+        spread = jnp.einsum("smik,slk->mil", placed_rows, col_pick, precision=exact)
+        own = spread[:, :tile_height, :tile_width]
+        from_left = from_offset(spread[:, :tile_height, tile_width:], "tile", -1) * keep_left
+        from_above = from_offset(spread[:, tile_height:, :tile_width], "tile", -GRID_X)
+        from_corner = (
+            from_offset(spread[:, tile_height:, tile_width:], "tile", -GRID_X - 1) * keep_left
+        )
+        maps = wave_sum(own + from_left + from_above + from_corner)
         largest = tile_max(jnp.max(maps[1]))
         tile_now = tile_now + 0.5 * maps[0] / (0.75 * maps[1] + 0.25 * largest)
     return tile_now[None]

time: 744 us -> 501 us (0.67)
  waiting for transfers between devices: 378 us -> 147 us
  local copies, waits for them, and re-layouts: 94.1 us -> 24.5 us
  blocking collectives: 98.5 us -> 163 us
  starting transfers between devices: 30.8 us -> 61.3 us
  matrix products: 8.8 us -> 33.2 us
  loops' own time: 22.4 us -> 0 us
  other arithmetic: 82.7 us -> 62.8 us
  between operations: 15.7 us -> 2.89 us
    psum x3 -> x0, waiting for transfers between devices: 258 us -> none  [shards(): numer_win, weight_win = lax.psum((numer_win, weight_win), 'wave')]
    all_to_all x3, blocking collectives: 98.5 us -> 163 us  [tile_max(): gathered = lax.all_to_all(spread, 'tile', 0, 0, tiled=True)]
    dynamic_update_slice x12 -> x0, local copies, waits for them, and re-layouts: 43.3 us -> none  [the longest x6 21.7 us: add_window(): lax.dynamic_update_slice(weight_map, lax.dynamic_slice(weight_map, (row_a...]
    ppermute x12 -> x30, starting transfers between devices: 30.8 us -> 61.3 us  [the longest x18 42.6 us: from_offset(): return lax.ppermute(block, axis, route)]
    ppermute x12 -> x30, waiting for transfers between devices: 119 us -> 147 us  [the longest x18 80.9 us: from_offset(): return lax.ppermute(block, axis, route)]
    dot_general x0 -> x12, matrix products: none -> 24.4 us  [the longest x3 10.7 us: shards(): spread = jnp.einsum('smik,slk->mil', placed_rows, col_pick, precision=exact)]
    another operation x6 -> x0, loops' own time: 22.4 us -> none  [the longest x3 22.2 us: shards(): numer_map, weight_map = lax.fori_loop(0, slots, add_window, (empty, empty))]
    gather x18 -> x0, local copies, waits for them, and re-layouts: 21.8 us -> none
  transfers between devices with their start and end apart: 15 -> 30, of which waited for: 15 -> 28; matrix products, arithmetic and copies ran while one was open for 3% -> 4% of each run, Pallas kernels for 0% -> 0%
where the time goes in v2:
time: 501 us; the launch traced here: 495 us
  blocking collectives  163 us (33%)
  waiting for transfers between devices  147 us (29%)
  other arithmetic  62.8 us (13%)
  starting transfers between devices  61.3 us (12%)
  matrix products  33.2 us (7%)
  local copies, waits for them, and re-layouts  24.5 us (5%)
    all_to_all x3, blocking collectives, tile_max(): gathered = lax.all_to_all(spread, 'tile', 0, 0, tiled=True)  163 us
    ppermute x18, waiting for transfers between devices, from_offset(): return lax.ppermute(block, axis, route)  80.9 us
    ppermute x12, waiting for transfers between devices, partner(): lax.ppermute(block, 'wave', [(i, i ^ bit) for i in range(lax.axis_size('w...  66 us
    ppermute x18, starting transfers between devices, from_offset(): return lax.ppermute(block, axis, route)  42.6 us
    ppermute x12, starting transfers between devices, partner(): lax.ppermute(block, 'wave', [(i, i ^ bit) for i in range(lax.axis_size('w...  18.7 us
    reduce_sum x3, other arithmetic, window_terms(): jnp.sum(slope_real * change_real + slope_imag * change_imag, axis=1)  17.9 us
    convert_element_type x3, other arithmetic, window_terms(): wave_real.astype(jnp.bfloat16)  13.6 us
    dot_general x3, matrix products, shards(): spread = jnp.einsum('smik,slk->mil', placed_rows, col_pick, precision=exact)  10.7 us
  transfers between devices with their start and end apart: 30, of which 28 were waited for; matrix products, arithmetic and copies ran while one was open for 4% of the time, Pallas kernels for 0%

profile of v2, /device:TPU:1, one launch (start us, length us, event | category | flops | bytes accessed | tf_op | source)
XLA Modules:
  0.0 494.7 jit_solution(5658379943549186196)
XLA Ops:
  18.7 7.0 %collective-permute-done.1 = f32[256,256]{1,0:T(8,128)} collective-permute-done((f32[256,256]{1,0:T(8,128)}, f32[256,256]{1,0:T(8,128)}, u32[]{:S(2)}, u32[]{:S(2)}) %collective-permute-start.1) | collective-permute-done | bytes 262176 | tf_op jit(solution)/shard_map/ppermute | solution.py:91
  28.8 4.6 fusion.216
  37.7 6.0 %fusion.44 = (f32[2,256,256]{2,1,0:T(8,128)}, f32[2,256,256]{2,1,0:T(8,128)}) fusion(f32[2,2,512,512]{3,2,1,0:T(8,128)S(1)} %fusion.68, f32[2]{0:T(128)S(1)} %copy-done.10, f32[2]{0:T(128)S(1)} %neg.15, f32[2,256,256]{2,1,0:T(8,128)S(1)} %get-tuple-element.58, f32[2,256,256]{2,1,0:T(8,128)S(1)} %fusion.133, f32[2,256,256]{2,1,0:T(8,128)S(1)} %get-tuple-element.57), kind=kLoop, calls=%fused_computation.73 | loop fusion | flops 7077888 | bytes 6815760 | tf_op jit(solution)/shard_map/reduce_sum | solution.py:76
  50.0 3.6 fusion.6
  57.5 5.6 %collective-permute-start.4 = (f32[2,256,256]{2,1,0:T(8,128)}, f32[2,256,256]{2,1,0:T(8,128)}, u32[]{:S(2)}, u32[]{:S(2)}) collective-permute-start(f32[2,256,256]{2,1,0:T(8,128)} %get-tuple-element.50), channel_id=1, source_target_pairs={{0,8},{1,9},{2,10},{3,11},{4,12},{5,13},{6,14},{7,15},{8,16},{9,17... | collective-permute-start | bytes 1572872 | tf_op jit(solution)/shard_map/ppermute | solution.py:91
  63.0 4.9 collective-permute-start.5
  68.3 4.6 collective-permute-done.4
  72.9 11.2 %collective-permute-done.5 = f32[2,256,256]{2,1,0:T(8,128)} collective-permute-done((f32[2,256,256]{2,1,0:T(8,128)}, f32[2,256,256]{2,1,0:T(8,128)}, u32[]{:S(2)}, u32[]{:S(2)}) %collective-permute-start.5) | collective-permute-done | bytes 524320 | tf_op jit(solution)/shard_map/ppermute | solution.py:91
  92.0 6.8 %collective-permute-done.7 = f32[2,128,256]{2,1,0:T(8,128)S(1)} collective-permute-done((f32[2,128,256]{2,1,0:T(8,128)S(1)}, f32[2,128,256]{2,1,0:T(8,128)S(1)}, u32[]{:S(2)}, u32[]{:S(2)}) %collective-permute-start.7) | collective-permute-done | bytes 262176 | tf_op jit(solution)/shard_map/ppermute | solution.py:95
  101.4 12.1 %collective-permute-done.8 = f32[2,128,256]{2,1,0:T(8,128)S(1)} collective-permute-done((f32[2,128,256]{2,1,0:T(8,128)S(1)}, f32[2,128,256]{2,1,0:T(8,128)S(1)}, u32[]{:S(2)}, u32[]{:S(2)}) %collective-permute-start.8) | collective-permute-done | bytes 262176 | tf_op jit(solution)/shard_map/ppermute | solution.py:95
  118.1 60.4 %all_to_all.18 = f32[32,1,128]{2,1,0:T(1,128)} all-to-all(f32[32,1,128]{2,1,0:T(1,128)S(1)} %broadcast_in_dim.6), channel_id=1, replica_groups=mesh['wave'=8,'tile'=32] {'tile'}, dimensions={0} | all-to-all | bytes 32768 | tf_op jit(solution)/shard_map/all_to_all | solution.py:84
  192.3 7.0 %collective-permute-done.10 = f32[256,256]{1,0:T(8,128)} collective-permute-done((f32[256,256]{1,0:T(8,128)}, f32[256,256]{1,0:T(8,128)}, u32[]{:S(2)}, u32[]{:S(2)}) %collective-permute-start.10) | collective-permute-done | bytes 262176 | tf_op jit(solution)/shard_map/ppermute | solution.py:91
  204.6 4.5 fusion.218
  213.3 6.0 %fusion.34 = (f32[2,256,256]{2,1,0:T(8,128)}, f32[2,256,256]{2,1,0:T(8,128)}) fusion(f32[2,2,512,512]{3,2,1,0:T(8,128)S(1)} %fusion.93, f32[2]{0:T(128)S(1)} %copy-done.10, f32[2]{0:T(128)S(1)} %neg.15, f32[2,256,256]{2,1,0:T(8,128)S(1)} %get-tuple-element.58, f32[2,256,256]{2,1,0:T(8,128)S(1)} %fusion.130, f32[2,256,256]{2,1,0:T(8,128)S(1)} %get-tuple-element.57), kind=kLoop, calls=%fused_computation.55 | loop fusion | flops 7077888 | bytes 6815760 | tf_op jit(solution)/shard_map/reduce_sum | solution.py:76
  225.7 3.6 fusion.9
  230.8 5.3 %collective-permute-start.14 = (f32[2,256,256]{2,1,0:T(8,128)S(1)}, f32[2,256,256]{2,1,0:T(8,128)S(1)}, u32[]{:S(2)}, u32[]{:S(2)}) collective-permute-start(f32[2,256,256]{2,1,0:T(8,128)S(1)} %get-tuple-element.47), channel_id=1, source_target_pairs={{0,8},{1,9},{2,10},{3,11},{4,12},{5,13},{6,14},{7,15},{8,16},{9,17... | collective-permute-start | bytes 1572872 | tf_op jit(solution)/shard_map/ppermute | solution.py:91
  237.5 8.4 %collective-permute-done.14 = f32[2,256,256]{2,1,0:T(8,128)S(1)} collective-permute-done((f32[2,256,256]{2,1,0:T(8,128)S(1)}, f32[2,256,256]{2,1,0:T(8,128)S(1)}, u32[]{:S(2)}, u32[]{:S(2)}) %collective-permute-start.14) | collective-permute-done | bytes 524320 | tf_op jit(solution)/shard_map/ppermute | solution.py:91
  245.9 11.2 %collective-permute-done.15 = f32[2,256,256]{2,1,0:T(8,128)S(1)} collective-permute-done((f32[2,256,256]{2,1,0:T(8,128)S(1)}, f32[2,256,256]{2,1,0:T(8,128)S(1)}, u32[]{:S(2)}, u32[]{:S(2)}) %collective-permute-start.15) | collective-permute-done | bytes 524320 | tf_op jit(solution)/shard_map/ppermute | solution.py:91
  261.2 7.5 %collective-permute-done.17 = f32[2,128,256]{2,1,0:T(8,128)S(1)} collective-permute-done((f32[2,128,256]{2,1,0:T(8,128)S(1)}, f32[2,128,256]{2,1,0:T(8,128)S(1)}, u32[]{:S(2)}, u32[]{:S(2)}) %collective-permute-start.17) | collective-permute-done | bytes 262176 | tf_op jit(solution)/shard_map/ppermute | solution.py:95
  271.3 11.5 %collective-permute-done.18 = f32[2,128,256]{2,1,0:T(8,128)S(1)} collective-permute-done((f32[2,128,256]{2,1,0:T(8,128)S(1)}, f32[2,128,256]{2,1,0:T(8,128)S(1)}, u32[]{:S(2)}, u32[]{:S(2)}) %collective-permute-start.18) | collective-permute-done | bytes 262176 | tf_op jit(solution)/shard_map/ppermute | solution.py:95
  287.0 51.5 %all_to_all.19 = f32[32,1,128]{2,1,0:T(1,128)} all-to-all(f32[32,1,128]{2,1,0:T(1,128)S(1)} %broadcast_in_dim.7), channel_id=1, replica_groups=mesh['wave'=8,'tile'=32] {'tile'}, dimensions={0} | all-to-all | bytes 32768 | tf_op jit(solution)/shard_map/all_to_all | solution.py:84
  349.0 6.2 %collective-permute-done.20 = f32[256,256]{1,0:T(8,128)} collective-permute-done((f32[256,256]{1,0:T(8,128)}, f32[256,256]{1,0:T(8,128)}, u32[]{:S(2)}, u32[]{:S(2)}) %collective-permute-start.20) | collective-permute-done | bytes 262176 | tf_op jit(solution)/shard_map/ppermute | solution.py:91
  360.2 4.5 fusion.220
  368.9 5.8 %fusion.24 = (f32[2,256,256]{2,1,0:T(8,128)}, f32[2,256,256]{2,1,0:T(8,128)S(1)}) fusion(f32[2,2,512,512]{3,2,1,0:T(8,128)S(1)} %fusion.118, f32[2]{0:T(128)S(1)} %copy-done.10, f32[2]{0:T(128)S(1)} %neg.15, f32[2,256,256]{2,1,0:T(8,128)S(1)} %get-tuple-element.58, f32[2,256,256]{2,1,0:T(8,128)S(1)} %fusion.127, f32[2,256,256]{2,1,0:T(8,128)S(1)} %get-tuple-element.57), kind=kLoop, calls=%fused_computation.37 | loop fusion | flops 7077888 | bytes 6815760 | tf_op jit(solution)/shard_map/reduce_sum | solution.py:76
  377.5 3.6 fusion.12
  381.3 4.5 collective-permute-start.23
  385.8 4.8 collective-permute-start.24
  395.1 4.6 collective-permute-done.24
  399.7 11.2 %collective-permute-done.25 = f32[2,256,256]{2,1,0:T(8,128)S(1)} collective-permute-done((f32[2,256,256]{2,1,0:T(8,128)S(1)}, f32[2,256,256]{2,1,0:T(8,128)S(1)}, u32[]{:S(2)}, u32[]{:S(2)}) %collective-permute-start.25) | collective-permute-done | bytes 524320 | tf_op jit(solution)/shard_map/ppermute | solution.py:91
  415.8 7.5 %collective-permute-done.27 = f32[2,128,256]{2,1,0:T(8,128)S(1)} collective-permute-done((f32[2,128,256]{2,1,0:T(8,128)S(1)}, f32[2,128,256]{2,1,0:T(8,128)S(1)}, u32[]{:S(2)}, u32[]{:S(2)}) %collective-permute-start.27) | collective-permute-done | bytes 262176 | tf_op jit(solution)/shard_map/ppermute | solution.py:95
  424.8 13.3 %collective-permute-done.28 = f32[2,128,256]{2,1,0:T(8,128)S(1)} collective-permute-done((f32[2,128,256]{2,1,0:T(8,128)S(1)}, f32[2,128,256]{2,1,0:T(8,128)S(1)}, u32[]{:S(2)}, u32[]{:S(2)}) %collective-permute-start.28) | collective-permute-done | bytes 262176 | tf_op jit(solution)/shard_map/ppermute | solution.py:95
  441.3 51.1 %all_to_all.20 = f32[32,1,128]{2,1,0:T(1,128)S(1)} all-to-all(f32[32,1,128]{2,1,0:T(1,128)S(1)} %broadcast_in_dim.8), channel_id=1, replica_groups=mesh['wave'=8,'tile'=32] {'tile'}, dimensions={0} | all-to-all | bytes 32768 | tf_op jit(solution)/shard_map/all_to_all | solution.py:84
  (178 shorter events, 131.3 us)
Async XLA Ops:
  0.0 13.4 %collective-permute-start.2 = (f32[256,256]{1,0:T(8,128)}, f32[256,256]{1,0:T(8,128)}, u32[]{:S(2)}, u32[]{:S(2)}) collective-permute-start(f32[256,256]{1,0:T(8,128)} %bitcast.136), channel_id=1, source_target_pairs={{9,0},{10,1},{11,2},{12,3},{13,4},{14,5},{15,6},{16,7},{17,8},{18,... | collective-permute-start | bytes 786440 | tf_op jit(solution)/shard_map/ppermute | solution.py:91
  1.5 16.3 %collective-permute-start = (f32[256,256]{1,0:T(8,128)}, f32[256,256]{1,0:T(8,128)}, u32[]{:S(2)}, u32[]{:S(2)}) collective-permute-start(f32[256,256]{1,0:T(8,128)} %bitcast.137), channel_id=1, source_target_pairs={{1,0},{2,1},{3,2},{4,3},{5,4},{6,5},{7,6},{8,7},{9,8},{10,9},{11,1... | collective-permute-start | bytes 786440 | tf_op jit(solution)/shard_map/ppermute | solution.py:91
  2.8 23.0 %collective-permute-start.1 = (f32[256,256]{1,0:T(8,128)}, f32[256,256]{1,0:T(8,128)}, u32[]{:S(2)}, u32[]{:S(2)}) collective-permute-start(f32[256,256]{1,0:T(8,128)} %bitcast.138), channel_id=1, source_target_pairs={{8,0},{9,1},{10,2},{11,3},{12,4},{13,5},{14,6},{15,7},{16,8},{17,9... | collective-permute-start | bytes 786440 | tf_op jit(solution)/shard_map/ppermute | solution.py:91
  56.1 12.1 %collective-permute-start.3 = (f32[2,256,256]{2,1,0:T(8,128)}, f32[2,256,256]{2,1,0:T(8,128)S(1)}, u32[]{:S(2)}, u32[]{:S(2)}) collective-permute-start(f32[2,256,256]{2,1,0:T(8,128)} %get-tuple-element.48), channel_id=1, source_target_pairs={{0,1},{1,2},{2,3},{3,4},{4,5},{5,6},{6,7},{7,8},{8,9},{9,10},{10,1... | collective-permute-start | bytes 1572872 | tf_op jit(solution)/shard_map/ppermute | solution.py:91
  57.5 15.4 %collective-permute-start.4 = (f32[2,256,256]{2,1,0:T(8,128)}, f32[2,256,256]{2,1,0:T(8,128)}, u32[]{:S(2)}, u32[]{:S(2)}) collective-permute-start(f32[2,256,256]{2,1,0:T(8,128)} %get-tuple-element.50), channel_id=1, source_target_pairs={{0,8},{1,9},{2,10},{3,11},{4,12},{5,13},{6,14},{7,15},{8,16},{9,17... | collective-permute-start | bytes 1572872 | tf_op jit(solution)/shard_map/ppermute | solution.py:91
  63.0 21.1 %collective-permute-start.5 = (f32[2,256,256]{2,1,0:T(8,128)}, f32[2,256,256]{2,1,0:T(8,128)}, u32[]{:S(2)}, u32[]{:S(2)}) collective-permute-start(f32[2,256,256]{2,1,0:T(8,128)} %get-tuple-element.49), channel_id=1, source_target_pairs={{0,9},{1,10},{2,11},{3,12},{4,13},{5,14},{6,15},{7,16},{8,17},{9,1... | collective-permute-start | bytes 1572872 | tf_op jit(solution)/shard_map/ppermute | solution.py:91
  86.5 3.7 collective-permute-start.6
  91.2 7.6 %collective-permute-start.7 = (f32[2,128,256]{2,1,0:T(8,128)S(1)}, f32[2,128,256]{2,1,0:T(8,128)S(1)}, u32[]{:S(2)}, u32[]{:S(2)}) collective-permute-start(f32[2,128,256]{2,1,0:T(8,128)S(1)} %dynamic-slice_add_fusion.2), channel_id=1, source_target_pairs={{0,64},{32,96},{64,0},{96,32},{128,192},{160,224},{192,128},{224,1... | collective-permute-start | bytes 786440 | tf_op jit(solution)/shard_map/ppermute | solution.py:95
  98.8 14.7 %collective-permute-start.8 = (f32[2,128,256]{2,1,0:T(8,128)S(1)}, f32[2,128,256]{2,1,0:T(8,128)S(1)}, u32[]{:S(2)}, u32[]{:S(2)}) collective-permute-start(f32[2,128,256]{2,1,0:T(8,128)S(1)} %add.341), channel_id=1, source_target_pairs={{0,128},{32,160},{64,192},{96,224},{128,0},{160,32},{192,64},{224,... | collective-permute-start | bytes 786440 | tf_op jit(solution)/shard_map/ppermute | solution.py:95
  113.6 2.2 collective-permute-start.9
  182.3 9.0 %collective-permute-start.12 = (f32[256,256]{1,0:T(8,128)}, f32[256,256]{1,0:T(8,128)}, u32[]{:S(2)}, u32[]{:S(2)}) collective-permute-start(f32[256,256]{1,0:T(8,128)} %get-tuple-element.22), channel_id=1, source_target_pairs={{9,0},{10,1},{11,2},{12,3},{13,4},{14,5},{15,6},{16,7},{17,8},{18,... | collective-permute-start | bytes 786440 | tf_op jit(solution)/shard_map/ppermute | solution.py:91
  184.8 14.4 %collective-permute-start.10 = (f32[256,256]{1,0:T(8,128)}, f32[256,256]{1,0:T(8,128)}, u32[]{:S(2)}, u32[]{:S(2)}) collective-permute-start(f32[256,256]{1,0:T(8,128)} %get-tuple-element.22), channel_id=1, source_target_pairs={{1,0},{2,1},{3,2},{4,3},{5,4},{6,5},{7,6},{8,7},{9,8},{10,9},{11,1... | collective-permute-start | bytes 786440 | tf_op jit(solution)/shard_map/ppermute | solution.py:91
  188.6 13.0 %collective-permute-start.11 = (f32[256,256]{1,0:T(8,128)}, f32[256,256]{1,0:T(8,128)S(1)}, u32[]{:S(2)}, u32[]{:S(2)}) collective-permute-start(f32[256,256]{1,0:T(8,128)} %get-tuple-element.22), channel_id=1, source_target_pairs={{8,0},{9,1},{10,2},{11,3},{12,4},{13,5},{14,6},{15,7},{16,8},{17,9... | collective-permute-start | bytes 786440 | tf_op jit(solution)/shard_map/ppermute | solution.py:91
  229.4 8.0 %collective-permute-start.13 = (f32[2,256,256]{2,1,0:T(8,128)S(1)}, f32[2,256,256]{2,1,0:T(8,128)S(1)}, u32[]{:S(2)}, u32[]{:S(2)}) collective-permute-start(f32[2,256,256]{2,1,0:T(8,128)S(1)} %get-tuple-element.45), channel_id=1, source_target_pairs={{0,1},{1,2},{2,3},{3,4},{4,5},{5,6},{6,7},{7,8},{8,9},{9,10},{10,1... | collective-permute-start | bytes 1572872 | tf_op jit(solution)/shard_map/ppermute | solution.py:91
  230.8 15.2 %collective-permute-start.14 = (f32[2,256,256]{2,1,0:T(8,128)S(1)}, f32[2,256,256]{2,1,0:T(8,128)S(1)}, u32[]{:S(2)}, u32[]{:S(2)}) collective-permute-start(f32[2,256,256]{2,1,0:T(8,128)S(1)} %get-tuple-element.47), channel_id=1, source_target_pairs={{0,8},{1,9},{2,10},{3,11},{4,12},{5,13},{6,14},{7,15},{8,16},{9,17... | collective-permute-start | bytes 1572872 | tf_op jit(solution)/shard_map/ppermute | solution.py:91
  236.1 21.1 %collective-permute-start.15 = (f32[2,256,256]{2,1,0:T(8,128)S(1)}, f32[2,256,256]{2,1,0:T(8,128)S(1)}, u32[]{:S(2)}, u32[]{:S(2)}) collective-permute-start(f32[2,256,256]{2,1,0:T(8,128)S(1)} %get-tuple-element.46), channel_id=1, source_target_pairs={{0,9},{1,10},{2,11},{3,12},{4,13},{5,14},{6,15},{7,16},{8,17},{9,1... | collective-permute-start | bytes 1572872 | tf_op jit(solution)/shard_map/ppermute | solution.py:91
  257.4 3.7 collective-permute-start.16
  261.1 7.6 %collective-permute-start.17 = (f32[2,128,256]{2,1,0:T(8,128)S(1)}, f32[2,128,256]{2,1,0:T(8,128)S(1)}, u32[]{:S(2)}, u32[]{:S(2)}) collective-permute-start(f32[2,128,256]{2,1,0:T(8,128)S(1)} %dynamic-slice_add_fusion.1), channel_id=1, source_target_pairs={{0,64},{32,96},{64,0},{96,32},{128,192},{160,224},{192,128},{224,1... | collective-permute-start | bytes 786440 | tf_op jit(solution)/shard_map/ppermute | solution.py:95
  268.7 14.1 %collective-permute-start.18 = (f32[2,128,256]{2,1,0:T(8,128)S(1)}, f32[2,128,256]{2,1,0:T(8,128)S(1)}, u32[]{:S(2)}, u32[]{:S(2)}) collective-permute-start(f32[2,128,256]{2,1,0:T(8,128)S(1)} %add.368), channel_id=1, source_target_pairs={{0,128},{32,160},{64,192},{96,224},{128,0},{160,32},{192,64},{224,... | collective-permute-start | bytes 786440 | tf_op jit(solution)/shard_map/ppermute | solution.py:95
  282.9 2.6 collective-permute-start.19
  342.2 12.9 %collective-permute-start.20 = (f32[256,256]{1,0:T(8,128)}, f32[256,256]{1,0:T(8,128)}, u32[]{:S(2)}, u32[]{:S(2)}) collective-permute-start(f32[256,256]{1,0:T(8,128)} %get-tuple-element.20), channel_id=1, source_target_pairs={{1,0},{2,1},{3,2},{4,3},{5,4},{6,5},{7,6},{8,7},{9,8},{10,9},{11,1... | collective-permute-start | bytes 786440 | tf_op jit(solution)/shard_map/ppermute | solution.py:91
  344.1 12.1 %collective-permute-start.22 = (f32[256,256]{1,0:T(8,128)}, f32[256,256]{1,0:T(8,128)}, u32[]{:S(2)}, u32[]{:S(2)}) collective-permute-start(f32[256,256]{1,0:T(8,128)} %get-tuple-element.20), channel_id=1, source_target_pairs={{9,0},{10,1},{11,2},{12,3},{13,4},{14,5},{15,6},{16,7},{17,8},{18,... | collective-permute-start | bytes 786440 | tf_op jit(solution)/shard_map/ppermute | solution.py:91
  347.7 9.6 %collective-permute-start.21 = (f32[256,256]{1,0:T(8,128)}, f32[256,256]{1,0:T(8,128)S(1)}, u32[]{:S(2)}, u32[]{:S(2)}) collective-permute-start(f32[256,256]{1,0:T(8,128)} %get-tuple-element.20), channel_id=1, source_target_pairs={{8,0},{9,1},{10,2},{11,3},{12,4},{13,5},{14,6},{15,7},{16,8},{17,9... | collective-permute-start | bytes 786440 | tf_op jit(solution)/shard_map/ppermute | solution.py:91
  381.3 13.8 %collective-permute-start.23 = (f32[2,256,256]{2,1,0:T(8,128)S(1)}, f32[2,256,256]{2,1,0:T(8,128)S(1)}, u32[]{:S(2)}, u32[]{:S(2)}) collective-permute-start(f32[2,256,256]{2,1,0:T(8,128)S(1)} %get-tuple-element.42), channel_id=1, source_target_pairs={{0,1},{1,2},{2,3},{3,4},{4,5},{5,6},{6,7},{7,8},{8,9},{9,10},{10,1... | collective-permute-start | bytes 1572872 | tf_op jit(solution)/shard_map/ppermute | solution.py:91
  385.8 13.9 %collective-permute-start.24 = (f32[2,256,256]{2,1,0:T(8,128)S(1)}, f32[2,256,256]{2,1,0:T(8,128)S(1)}, u32[]{:S(2)}, u32[]{:S(2)}) collective-permute-start(f32[2,256,256]{2,1,0:T(8,128)S(1)} %get-tuple-element.44), channel_id=1, source_target_pairs={{0,8},{1,9},{2,10},{3,11},{4,12},{5,13},{6,14},{7,15},{8,16},{9,17... | collective-permute-start | bytes 1572872 | tf_op jit(solution)/shard_map/ppermute | solution.py:91
  390.6 20.4 %collective-permute-start.25 = (f32[2,256,256]{2,1,0:T(8,128)S(1)}, f32[2,256,256]{2,1,0:T(8,128)S(1)}, u32[]{:S(2)}, u32[]{:S(2)}) collective-permute-start(f32[2,256,256]{2,1,0:T(8,128)S(1)} %get-tuple-element.43), channel_id=1, source_target_pairs={{0,9},{1,10},{2,11},{3,12},{4,13},{5,14},{6,15},{7,16},{8,17},{9,1... | collective-permute-start | bytes 1572872 | tf_op jit(solution)/shard_map/ppermute | solution.py:91
  411.2 82.5 %copy-start.5 = (f32[1,256,256]{2,1,0:T(8,128)S(1)}, f32[1,256,256]{2,1,0:T(8,128)}, u32[]{:S(2)}) copy-start(f32[1,256,256]{2,1,0:T(8,128)} %param.8) | copy-start | bytes 786436
  411.2 82.5 %copy-start.6 = (f32[1,256,256]{2,1,0:T(8,128)S(1)}, f32[1,256,256]{2,1,0:T(8,128)}, u32[]{:S(2)}) copy-start(f32[1,256,256]{2,1,0:T(8,128)} %get-tuple-element.23) | copy-start | bytes 786436
  411.2 4.4 collective-permute-start.26
  415.7 7.6 %collective-permute-start.27 = (f32[2,128,256]{2,1,0:T(8,128)S(1)}, f32[2,128,256]{2,1,0:T(8,128)S(1)}, u32[]{:S(2)}, u32[]{:S(2)}) collective-permute-start(f32[2,128,256]{2,1,0:T(8,128)S(1)} %dynamic-slice_add_fusion), channel_id=1, source_target_pairs={{0,64},{32,96},{64,0},{96,32},{128,192},{160,224},{192,128},{224,1... | collective-permute-start | bytes 786440 | tf_op jit(solution)/shard_map/ppermute | solution.py:95
  423.3 14.8 %collective-permute-start.28 = (f32[2,128,256]{2,1,0:T(8,128)S(1)}, f32[2,128,256]{2,1,0:T(8,128)S(1)}, u32[]{:S(2)}, u32[]{:S(2)}) collective-permute-start(f32[2,128,256]{2,1,0:T(8,128)S(1)} %add.395), channel_id=1, source_target_pairs={{0,128},{32,160},{64,192},{96,224},{128,0},{160,32},{192,64},{224,... | collective-permute-start | bytes 786440 | tf_op jit(solution)/shard_map/ppermute | solution.py:95
  438.1 1.7 collective-permute-start.29
  (17 other events, 168.2 us)

commit v3 on v2

--- a/solution.py
+++ b/solution.py
@@ -128,13 +128,13 @@
     keep_left = (column != 0).astype(jnp.float32)
     cos_table, sin_table = tables(window)
     exact = lax.Precision.HIGHEST
+    right = from_offset(tile_now, "tile", 1) * keep_right
+    below = from_offset(tile_now, "tile", GRID_X)
+    corner = from_offset(tile_now, "tile", GRID_X + 1) * keep_right
+    extended = jnp.concatenate(
+        [jnp.concatenate([tile_now, right], 1), jnp.concatenate([below, corner], 1)], 0
+    )
     for batch_index in range(BATCHES):
-        right = from_offset(tile_now, "tile", 1) * keep_right
-        below = from_offset(tile_now, "tile", GRID_X)
-        corner = from_offset(tile_now, "tile", GRID_X + 1) * keep_right
-        extended = jnp.concatenate(
-            [jnp.concatenate([tile_now, right], 1), jnp.concatenate([below, corner], 1)], 0
-        )
         chosen = batch_order[0, batch_index * slots : (batch_index + 1) * slots]
         places = positions[0][chosen]
         measured = amplitudes[0][chosen]
@@ -156,8 +156,23 @@
             from_offset(spread[:, tile_height:, tile_width:], "tile", -GRID_X - 1) * keep_left
         )
         maps = wave_sum(own + from_left + from_above + from_corner)
-        largest = tile_max(jnp.max(maps[1]))
-        tile_now = tile_now + 0.5 * maps[0] / (0.75 * maps[1] + 0.25 * largest)
+        if batch_index + 1 < BATCHES:
+            maps_right = from_offset(maps, "tile", 1) * keep_right
+            maps_below = from_offset(maps, "tile", GRID_X)
+            maps_corner = from_offset(maps, "tile", GRID_X + 1) * keep_right
+            maps = jnp.concatenate(
+                [
+                    jnp.concatenate([maps, maps_right], 2),
+                    jnp.concatenate([maps_below, maps_corner], 2),
+                ],
+                1,
+            )
+        largest = tile_max(jnp.max(maps[1, :tile_height, :tile_width]))
+        if batch_index + 1 < BATCHES:
+            extended = extended + 0.5 * maps[0] / (0.75 * maps[1] + 0.25 * largest)
+            tile_now = extended[:tile_height, :tile_width]
+        else:
+            tile_now = tile_now + 0.5 * maps[0] / (0.75 * maps[1] + 0.25 * largest)
     return tile_now[None]
 
 

time: 501 us -> 518 us (1.034)
  blocking collectives: 163 us -> 45.8 us
  starting transfers between devices: 61.3 us -> 150 us
  waiting for transfers between devices: 147 us -> 184 us
  local copies, waits for them, and re-layouts: 24.5 us -> 31.3 us
    all_to_all x3 -> x1, blocking collectives: 163 us -> 45.8 us  [tile_max(): gathered = lax.all_to_all(spread, 'tile', 0, 0, tiled=True)]
    all_to_all x0 -> x2, starting transfers between devices: none -> 97.5 us  [tile_max(): gathered = lax.all_to_all(spread, 'tile', 0, 0, tiled=True)]
    all_to_all x0 -> x2, waiting for transfers between devices: none -> 51.1 us  [tile_max(): gathered = lax.all_to_all(spread, 'tile', 0, 0, tiled=True)]
    ppermute x18, waiting for transfers between devices: 80.9 us -> 63 us  [from_offset(): return lax.ppermute(block, axis, route)]
    ppermute x12, starting transfers between devices: 18.7 us -> 12.8 us  [partner(): lax.ppermute(block, 'wave', [(i, i ^ bit) for i in range(lax.axis_size('w...]
  transfers between devices with their start and end apart: 30 -> 32, of which waited for: 28 -> 25; matrix products, arithmetic and copies ran while one was open for 4% -> 7% of each run, Pallas kernels for 0% -> 0%
where the time goes in v3:
time: 518 us; the launch traced here: 511 us
  waiting for transfers between devices  184 us (36%)
  starting transfers between devices  150 us (29%)
  other arithmetic  66.9 us (13%)
  blocking collectives  45.8 us (9%)
  local copies, waits for them, and re-layouts  31.3 us (6%)
  matrix products  30.7 us (6%)
    all_to_all x2, starting transfers between devices, tile_max(): gathered = lax.all_to_all(spread, 'tile', 0, 0, tiled=True)  97.5 us
    ppermute x12, waiting for transfers between devices, partner(): lax.ppermute(block, 'wave', [(i, i ^ bit) for i in range(lax.axis_size('w...  69.9 us
    ppermute x18, waiting for transfers between devices, from_offset(): return lax.ppermute(block, axis, route)  63 us
    all_to_all x2, waiting for transfers between devices, tile_max(): gathered = lax.all_to_all(spread, 'tile', 0, 0, tiled=True)  51.1 us
    all_to_all x1, blocking collectives, tile_max(): gathered = lax.all_to_all(spread, 'tile', 0, 0, tiled=True)  45.8 us
    ppermute x18, starting transfers between devices, from_offset(): return lax.ppermute(block, axis, route)  39.3 us
    reduce_sum x3, other arithmetic, window_terms(): jnp.sum(slope_real * change_real + slope_imag * change_imag, axis=1)  17.9 us
    convert_element_type x3, other arithmetic, window_terms(): wave_real.astype(jnp.bfloat16)  13.9 us
  transfers between devices with their start and end apart: 32, of which 25 were waited for; matrix products, arithmetic and copies ran while one was open for 7% of the time, Pallas kernels for 0%

profile of v3, /device:TPU:1, one launch (start us, length us, event | category | flops | bytes accessed | tf_op | source)
XLA Modules:
  0.0 511.4 jit_solution(7633520855794515349)
XLA Ops:
  14.4 3.3 collective-permute-done
  18.7 7.0 %collective-permute-done.1 = f32[256,256]{1,0:T(8,128)} collective-permute-done((f32[256,256]{1,0:T(8,128)}, f32[256,256]{1,0:T(8,128)}, u32[]{:S(2)}, u32[]{:S(2)}) %collective-permute-start.1) | collective-permute-done | bytes 262176 | tf_op jit(solution)/shard_map/ppermute | solution.py:91
  28.8 5.0 fusion.205
  38.0 6.0 %fusion.52 = (f32[2,256,256]{2,1,0:T(8,128)}, f32[2,256,256]{2,1,0:T(8,128)}) fusion(f32[2,2,512,512]{3,2,1,0:T(8,128)S(1)} %fusion.69, f32[2]{0:T(128)S(1)} %copy-done.15, f32[2]{0:T(128)S(1)} %neg.15, f32[2,256,256]{2,1,0:T(8,128)S(1)} %get-tuple-element.54, f32[2,256,256]{2,1,0:T(8,128)S(1)} %fusion.126, f32[2,256,256]{2,1,0:T(8,128)S(1)} %get-tuple-element.53), kind=kLoop, calls=%fused_computation.87 | loop fusion | flops 7077888 | bytes 6815760 | tf_op jit(solution)/shard_map/reduce_sum | solution.py:76
  50.4 3.6 fusion.6
  57.9 5.8 %collective-permute-start.4 = (f32[2,256,256]{2,1,0:T(8,128)}, f32[2,256,256]{2,1,0:T(8,128)}, u32[]{:S(2)}, u32[]{:S(2)}) collective-permute-start(f32[2,256,256]{2,1,0:T(8,128)} %get-tuple-element.46), channel_id=1, source_target_pairs={{0,8},{1,9},{2,10},{3,11},{4,12},{5,13},{6,14},{7,15},{8,16},{9,17... | collective-permute-start | bytes 1572872 | tf_op jit(solution)/shard_map/ppermute | solution.py:91
  63.7 4.9 collective-permute-start.5
  68.7 4.8 collective-permute-done.4
  73.6 11.2 %collective-permute-done.5 = f32[2,256,256]{2,1,0:T(8,128)} collective-permute-done((f32[2,256,256]{2,1,0:T(8,128)}, f32[2,256,256]{2,1,0:T(8,128)}, u32[]{:S(2)}, u32[]{:S(2)}) %collective-permute-start.5) | collective-permute-done | bytes 524320 | tf_op jit(solution)/shard_map/ppermute | solution.py:91
  92.4 6.8 %collective-permute-done.7 = f32[2,128,256]{2,1,0:T(8,128)S(1)} collective-permute-done((f32[2,128,256]{2,1,0:T(8,128)S(1)}, f32[2,128,256]{2,1,0:T(8,128)S(1)}, u32[]{:S(2)}, u32[]{:S(2)}) %collective-permute-start.7) | collective-permute-done | bytes 262176 | tf_op jit(solution)/shard_map/ppermute | solution.py:95
  101.7 12.0 %collective-permute-done.8 = f32[2,128,256]{2,1,0:T(8,128)S(1)} collective-permute-done((f32[2,128,256]{2,1,0:T(8,128)S(1)}, f32[2,128,256]{2,1,0:T(8,128)S(1)}, u32[]{:S(2)}, u32[]{:S(2)}) %collective-permute-start.8) | collective-permute-done | bytes 262176 | tf_op jit(solution)/shard_map/ppermute | solution.py:95
  125.6 55.1 %all-to-all-start = ((f32[32,1,128]{2,1,0:T(1,128)}), f32[32,1,128]{2,1,0:T(1,128)}, u32[]{:S(2)}, u32[]{:S(2)}) async-start(f32[32,1,128]{2,1,0:T(1,128)} %broadcast_in_dim.8), calls=%async_computation | async-start | bytes 32768 | tf_op jit(solution)/shard_map/all_to_all | solution.py:84
  185.0 25.8 %all-to-all-done = f32[32,1,128]{2,1,0:T(1,128)} async-done(((f32[32,1,128]{2,1,0:T(1,128)}), f32[32,1,128]{2,1,0:T(1,128)}, u32[]{:S(2)}, u32[]{:S(2)}) %all-to-all-start) | async-done | bytes 16416 | tf_op jit(solution)/shard_map/all_to_all | solution.py:84
  219.8 4.5 fusion.207
  228.5 6.0 %fusion.38 = (f32[2,256,256]{2,1,0:T(8,128)}, f32[2,256,256]{2,1,0:T(8,128)}) fusion(f32[2,2,512,512]{3,2,1,0:T(8,128)S(1)} %fusion.87, f32[2]{0:T(128)S(1)} %copy-done.15, f32[2]{0:T(128)S(1)} %neg.15, f32[2,256,256]{2,1,0:T(8,128)S(1)} %get-tuple-element.54, f32[2,256,256]{2,1,0:T(8,128)S(1)} %fusion.123, f32[2,256,256]{2,1,0:T(8,128)S(1)} %get-tuple-element.53), kind=kLoop, calls=%fused_computation.63 | loop fusion | flops 7077888 | bytes 6815760 | tf_op jit(solution)/shard_map/reduce_sum | solution.py:76
  240.2 3.6 fusion.9
  243.9 3.2 collective-permute-start.13
  251.8 5.5 %collective-permute-done.13 = f32[2,256,256]{2,1,0:T(8,128)S(1)} collective-permute-done((f32[2,256,256]{2,1,0:T(8,128)S(1)}, f32[2,256,256]{2,1,0:T(8,128)S(1)}, u32[]{:S(2)}, u32[]{:S(2)}) %collective-permute-start.13) | collective-permute-done | bytes 524320 | tf_op jit(solution)/shard_map/ppermute | solution.py:91
  258.6 11.2 %collective-permute-done.15 = f32[2,256,256]{2,1,0:T(8,128)S(1)} collective-permute-done((f32[2,256,256]{2,1,0:T(8,128)S(1)}, f32[2,256,256]{2,1,0:T(8,128)S(1)}, u32[]{:S(2)}, u32[]{:S(2)}) %collective-permute-start.15) | collective-permute-done | bytes 524320 | tf_op jit(solution)/shard_map/ppermute | solution.py:91
  273.7 7.5 %collective-permute-done.17 = f32[2,128,256]{2,1,0:T(8,128)S(1)} collective-permute-done((f32[2,128,256]{2,1,0:T(8,128)S(1)}, f32[2,128,256]{2,1,0:T(8,128)S(1)}, u32[]{:S(2)}, u32[]{:S(2)}) %collective-permute-start.17) | collective-permute-done | bytes 262176 | tf_op jit(solution)/shard_map/ppermute | solution.py:95
  281.3 14.7 %collective-permute-done.18 = f32[2,128,256]{2,1,0:T(8,128)S(1)} collective-permute-done((f32[2,128,256]{2,1,0:T(8,128)S(1)}, f32[2,128,256]{2,1,0:T(8,128)S(1)}, u32[]{:S(2)}, u32[]{:S(2)}) %collective-permute-start.18) | collective-permute-done | bytes 262176 | tf_op jit(solution)/shard_map/ppermute | solution.py:95
  305.7 42.4 %all-to-all-start.1 = ((f32[32,1,128]{2,1,0:T(1,128)}), f32[32,1,128]{2,1,0:T(1,128)S(1)}, u32[]{:S(2)}, u32[]{:S(2)}) async-start(f32[32,1,128]{2,1,0:T(1,128)} %broadcast_in_dim.9), calls=%async_computation.1 | async-start | bytes 32768 | tf_op jit(solution)/shard_map/all_to_all | solution.py:84
  353.3 25.3 %all-to-all-done.1 = f32[32,1,128]{2,1,0:T(1,128)S(1)} async-done(((f32[32,1,128]{2,1,0:T(1,128)}), f32[32,1,128]{2,1,0:T(1,128)S(1)}, u32[]{:S(2)}, u32[]{:S(2)}) %all-to-all-start.1) | async-done | bytes 16416 | tf_op jit(solution)/shard_map/all_to_all | solution.py:84
  386.1 4.5 fusion.209
  394.8 5.9 %fusion.24 = (f32[2,256,256]{2,1,0:T(8,128)}, f32[2,256,256]{2,1,0:T(8,128)S(1)}) fusion(f32[2,2,512,512]{3,2,1,0:T(8,128)S(1)} %fusion.105, f32[2]{0:T(128)S(1)} %copy-done.16, f32[2]{0:T(128)S(1)} %copy-done.18, f32[2,256,256]{2,1,0:T(8,128)S(1)} %get-tuple-element.54, f32[2,256,256]{2,1,0:T(8,128)S(1)} %fusion.120, f32[2,256,256]{2,1,0:T(8,128)S(1)} %get-tuple-element.53), kind=kLoop, calls=%fused_computation.39 | loop fusion | flops 7077888 | bytes 6815760 | tf_op jit(solution)/shard_map/reduce_sum | solution.py:76
  403.5 3.6 fusion.12
  407.2 3.2 collective-permute-start.23
  415.0 5.9 %collective-permute-done.23 = f32[2,256,256]{2,1,0:T(8,128)S(1)} collective-permute-done((f32[2,256,256]{2,1,0:T(8,128)S(1)}, f32[2,256,256]{2,1,0:T(8,128)S(1)}, u32[]{:S(2)}, u32[]{:S(2)}) %collective-permute-start.23) | collective-permute-done | bytes 524320 | tf_op jit(solution)/shard_map/ppermute | solution.py:91
  422.2 11.2 %collective-permute-done.25 = f32[2,256,256]{2,1,0:T(8,128)S(1)} collective-permute-done((f32[2,256,256]{2,1,0:T(8,128)S(1)}, f32[2,256,256]{2,1,0:T(8,128)S(1)}, u32[]{:S(2)}, u32[]{:S(2)}) %collective-permute-start.25) | collective-permute-done | bytes 524320 | tf_op jit(solution)/shard_map/ppermute | solution.py:91
  436.9 7.5 %collective-permute-done.27 = f32[2,128,256]{2,1,0:T(8,128)S(1)} collective-permute-done((f32[2,128,256]{2,1,0:T(8,128)S(1)}, f32[2,128,256]{2,1,0:T(8,128)S(1)}, u32[]{:S(2)}, u32[]{:S(2)}) %collective-permute-start.27) | collective-permute-done | bytes 262176 | tf_op jit(solution)/shard_map/ppermute | solution.py:95
  445.2 14.0 %collective-permute-done.28 = f32[2,128,256]{2,1,0:T(8,128)S(1)} collective-permute-done((f32[2,128,256]{2,1,0:T(8,128)S(1)}, f32[2,128,256]{2,1,0:T(8,128)S(1)}, u32[]{:S(2)}, u32[]{:S(2)}) %collective-permute-start.28) | collective-permute-done | bytes 262176 | tf_op jit(solution)/shard_map/ppermute | solution.py:95
  462.4 45.8 %all_to_all.18 = f32[32,1,128]{2,1,0:T(1,128)S(1)} all-to-all(f32[32,1,128]{2,1,0:T(1,128)S(1)} %broadcast_in_dim.10), channel_id=1, replica_groups=mesh['wave'=8,'tile'=32] {'tile'}, dimensions={0} | all-to-all | bytes 32768 | tf_op jit(solution)/shard_map/all_to_all | solution.py:84
  (206 shorter events, 131.4 us)
Async XLA Ops:
  0.0 13.4 %collective-permute-start.2 = (f32[256,256]{1,0:T(8,128)}, f32[256,256]{1,0:T(8,128)}, u32[]{:S(2)}, u32[]{:S(2)}) collective-permute-start(f32[256,256]{1,0:T(8,128)} %bitcast.147), channel_id=1, source_target_pairs={{9,0},{10,1},{11,2},{12,3},{13,4},{14,5},{15,6},{16,7},{17,8},{18,... | collective-permute-start | bytes 786440 | tf_op jit(solution)/shard_map/ppermute | solution.py:91
  1.5 16.3 %collective-permute-start = (f32[256,256]{1,0:T(8,128)}, f32[256,256]{1,0:T(8,128)}, u32[]{:S(2)}, u32[]{:S(2)}) collective-permute-start(f32[256,256]{1,0:T(8,128)} %bitcast.148), channel_id=1, source_target_pairs={{1,0},{2,1},{3,2},{4,3},{5,4},{6,5},{7,6},{8,7},{9,8},{10,9},{11,1... | collective-permute-start | bytes 786440 | tf_op jit(solution)/shard_map/ppermute | solution.py:91
  2.8 23.0 %collective-permute-start.1 = (f32[256,256]{1,0:T(8,128)}, f32[256,256]{1,0:T(8,128)}, u32[]{:S(2)}, u32[]{:S(2)}) collective-permute-start(f32[256,256]{1,0:T(8,128)} %bitcast.149), channel_id=1, source_target_pairs={{8,0},{9,1},{10,2},{11,3},{12,4},{13,5},{14,6},{15,7},{16,8},{17,9... | collective-permute-start | bytes 786440 | tf_op jit(solution)/shard_map/ppermute | solution.py:91
  56.6 12.1 %collective-permute-start.3 = (f32[2,256,256]{2,1,0:T(8,128)}, f32[2,256,256]{2,1,0:T(8,128)S(1)}, u32[]{:S(2)}, u32[]{:S(2)}) collective-permute-start(f32[2,256,256]{2,1,0:T(8,128)} %get-tuple-element.44), channel_id=1, source_target_pairs={{0,1},{1,2},{2,3},{3,4},{4,5},{5,6},{6,7},{7,8},{8,9},{9,10},{10,1... | collective-permute-start | bytes 1572872 | tf_op jit(solution)/shard_map/ppermute | solution.py:91
  57.9 15.7 %collective-permute-start.4 = (f32[2,256,256]{2,1,0:T(8,128)}, f32[2,256,256]{2,1,0:T(8,128)}, u32[]{:S(2)}, u32[]{:S(2)}) collective-permute-start(f32[2,256,256]{2,1,0:T(8,128)} %get-tuple-element.46), channel_id=1, source_target_pairs={{0,8},{1,9},{2,10},{3,11},{4,12},{5,13},{6,14},{7,15},{8,16},{9,17... | collective-permute-start | bytes 1572872 | tf_op jit(solution)/shard_map/ppermute | solution.py:91
  63.7 21.1 %collective-permute-start.5 = (f32[2,256,256]{2,1,0:T(8,128)}, f32[2,256,256]{2,1,0:T(8,128)}, u32[]{:S(2)}, u32[]{:S(2)}) collective-permute-start(f32[2,256,256]{2,1,0:T(8,128)} %get-tuple-element.45), channel_id=1, source_target_pairs={{0,9},{1,10},{2,11},{3,12},{4,13},{5,14},{6,15},{7,16},{8,17},{9,1... | collective-permute-start | bytes 1572872 | tf_op jit(solution)/shard_map/ppermute | solution.py:91
  87.2 3.5 collective-permute-start.6
  91.6 7.6 %collective-permute-start.7 = (f32[2,128,256]{2,1,0:T(8,128)S(1)}, f32[2,128,256]{2,1,0:T(8,128)S(1)}, u32[]{:S(2)}, u32[]{:S(2)}) collective-permute-start(f32[2,128,256]{2,1,0:T(8,128)S(1)} %dynamic-slice_add_fusion.2), channel_id=1, source_target_pairs={{0,64},{32,96},{64,0},{96,32},{128,192},{160,224},{192,128},{224,1... | collective-permute-start | bytes 786440 | tf_op jit(solution)/shard_map/ppermute | solution.py:95
  99.2 14.4 %collective-permute-start.8 = (f32[2,128,256]{2,1,0:T(8,128)S(1)}, f32[2,128,256]{2,1,0:T(8,128)S(1)}, u32[]{:S(2)}, u32[]{:S(2)}) collective-permute-start(f32[2,128,256]{2,1,0:T(8,128)S(1)} %add.332), channel_id=1, source_target_pairs={{0,128},{32,160},{64,192},{96,224},{128,0},{160,32},{192,64},{224,... | collective-permute-start | bytes 786440 | tf_op jit(solution)/shard_map/ppermute | solution.py:95
  113.7 2.3 collective-permute-start.9
  118.0 94.9 %collective-permute-start.10 = (f32[2,256,256]{2,1,0:T(8,128)}, f32[2,256,256]{2,1,0:T(8,128)}, u32[]{:S(2)}, u32[]{:S(2)}) collective-permute-start(f32[2,256,256]{2,1,0:T(8,128)} %pad_maximum_fusion), channel_id=1, source_target_pairs={{1,0},{2,1},{3,2},{4,3},{5,4},{6,5},{7,6},{8,7},{9,8},{10,9},{11,1... | collective-permute-start | bytes 1572872 | tf_op jit(solution)/shard_map/ppermute | solution.py:91
  119.2 94.7 %collective-permute-start.12 = (f32[2,256,256]{2,1,0:T(8,128)}, f32[2,256,256]{2,1,0:T(8,128)}, u32[]{:S(2)}, u32[]{:S(2)}) collective-permute-start(f32[2,256,256]{2,1,0:T(8,128)} %pad_maximum_fusion), channel_id=1, source_target_pairs={{9,0},{10,1},{11,2},{12,3},{13,4},{14,5},{15,6},{16,7},{17,8},{18,... | collective-permute-start | bytes 1572872 | tf_op jit(solution)/shard_map/ppermute | solution.py:91
  122.5 92.6 %collective-permute-start.11 = (f32[2,256,256]{2,1,0:T(8,128)}, f32[2,256,256]{2,1,0:T(8,128)}, u32[]{:S(2)}, u32[]{:S(2)}) collective-permute-start(f32[2,256,256]{2,1,0:T(8,128)} %pad_maximum_fusion), channel_id=1, source_target_pairs={{8,0},{9,1},{10,2},{11,3},{12,4},{13,5},{14,6},{15,7},{16,8},{17,9... | collective-permute-start | bytes 1572872 | tf_op jit(solution)/shard_map/ppermute | solution.py:91
  125.6 85.2 %all-to-all-start = ((f32[32,1,128]{2,1,0:T(1,128)}), f32[32,1,128]{2,1,0:T(1,128)}, u32[]{:S(2)}, u32[]{:S(2)}) async-start(f32[32,1,128]{2,1,0:T(1,128)} %broadcast_in_dim.8), calls=%async_computation | async-start | bytes 32768 | tf_op jit(solution)/shard_map/all_to_all | solution.py:84
  243.9 13.4 %collective-permute-start.13 = (f32[2,256,256]{2,1,0:T(8,128)S(1)}, f32[2,256,256]{2,1,0:T(8,128)S(1)}, u32[]{:S(2)}, u32[]{:S(2)}) collective-permute-start(f32[2,256,256]{2,1,0:T(8,128)S(1)} %get-tuple-element.41), channel_id=1, source_target_pairs={{0,1},{1,2},{2,3},{3,4},{4,5},{5,6},{6,7},{7,8},{8,9},{9,10},{10,1... | collective-permute-start | bytes 1572872 | tf_op jit(solution)/shard_map/ppermute | solution.py:91
  247.2 11.5 %collective-permute-start.14 = (f32[2,256,256]{2,1,0:T(8,128)S(1)}, f32[2,256,256]{2,1,0:T(8,128)S(1)}, u32[]{:S(2)}, u32[]{:S(2)}) collective-permute-start(f32[2,256,256]{2,1,0:T(8,128)S(1)} %get-tuple-element.43), channel_id=1, source_target_pairs={{0,8},{1,9},{2,10},{3,11},{4,12},{5,13},{6,14},{7,15},{8,16},{9,17... | collective-permute-start | bytes 1572872 | tf_op jit(solution)/shard_map/ppermute | solution.py:91
  248.8 21.1 %collective-permute-start.15 = (f32[2,256,256]{2,1,0:T(8,128)S(1)}, f32[2,256,256]{2,1,0:T(8,128)S(1)}, u32[]{:S(2)}, u32[]{:S(2)}) collective-permute-start(f32[2,256,256]{2,1,0:T(8,128)S(1)} %get-tuple-element.42), channel_id=1, source_target_pairs={{0,9},{1,10},{2,11},{3,12},{4,13},{5,14},{6,15},{7,16},{8,17},{9,1... | collective-permute-start | bytes 1572872 | tf_op jit(solution)/shard_map/ppermute | solution.py:91
  270.1 3.5 collective-permute-start.16
  273.6 7.6 %collective-permute-start.17 = (f32[2,128,256]{2,1,0:T(8,128)S(1)}, f32[2,128,256]{2,1,0:T(8,128)S(1)}, u32[]{:S(2)}, u32[]{:S(2)}) collective-permute-start(f32[2,128,256]{2,1,0:T(8,128)S(1)} %dynamic-slice_add_fusion.1), channel_id=1, source_target_pairs={{0,64},{32,96},{64,0},{96,32},{128,192},{160,224},{192,128},{224,1... | collective-permute-start | bytes 786440 | tf_op jit(solution)/shard_map/ppermute | solution.py:95
  281.2 14.8 %collective-permute-start.18 = (f32[2,128,256]{2,1,0:T(8,128)S(1)}, f32[2,128,256]{2,1,0:T(8,128)S(1)}, u32[]{:S(2)}, u32[]{:S(2)}) collective-permute-start(f32[2,128,256]{2,1,0:T(8,128)S(1)} %add.358), channel_id=1, source_target_pairs={{0,128},{32,160},{64,192},{96,224},{128,0},{160,32},{192,64},{224,... | collective-permute-start | bytes 786440 | tf_op jit(solution)/shard_map/ppermute | solution.py:95
  296.1 1.7 collective-permute-start.19
  298.7 81.1 %collective-permute-start.20 = (f32[2,256,256]{2,1,0:T(8,128)}, f32[2,256,256]{2,1,0:T(8,128)}, u32[]{:S(2)}, u32[]{:S(2)}) collective-permute-start(f32[2,256,256]{2,1,0:T(8,128)} %pad_maximum_fusion.1), channel_id=1, source_target_pairs={{1,0},{2,1},{3,2},{4,3},{5,4},{6,5},{7,6},{8,7},{9,8},{10,9},{11,1... | collective-permute-start | bytes 1572872 | tf_op jit(solution)/shard_map/ppermute | solution.py:91
  300.0 80.9 %collective-permute-start.22 = (f32[2,256,256]{2,1,0:T(8,128)}, f32[2,256,256]{2,1,0:T(8,128)}, u32[]{:S(2)}, u32[]{:S(2)}) collective-permute-start(f32[2,256,256]{2,1,0:T(8,128)} %pad_maximum_fusion.1), channel_id=1, source_target_pairs={{9,0},{10,1},{11,2},{12,3},{13,4},{14,5},{15,6},{16,7},{17,8},{18,... | collective-permute-start | bytes 1572872 | tf_op jit(solution)/shard_map/ppermute | solution.py:91
  302.6 79.4 %collective-permute-start.21 = (f32[2,256,256]{2,1,0:T(8,128)}, f32[2,256,256]{2,1,0:T(8,128)}, u32[]{:S(2)}, u32[]{:S(2)}) collective-permute-start(f32[2,256,256]{2,1,0:T(8,128)} %pad_maximum_fusion.1), channel_id=1, source_target_pairs={{8,0},{9,1},{10,2},{11,3},{12,4},{13,5},{14,6},{15,7},{16,8},{17,9... | collective-permute-start | bytes 1572872 | tf_op jit(solution)/shard_map/ppermute | solution.py:91
  305.7 72.8 %all-to-all-start.1 = ((f32[32,1,128]{2,1,0:T(1,128)}), f32[32,1,128]{2,1,0:T(1,128)S(1)}, u32[]{:S(2)}, u32[]{:S(2)}) async-start(f32[32,1,128]{2,1,0:T(1,128)} %broadcast_in_dim.9), calls=%async_computation.1 | async-start | bytes 32768 | tf_op jit(solution)/shard_map/all_to_all | solution.py:84
  407.2 13.7 %collective-permute-start.23 = (f32[2,256,256]{2,1,0:T(8,128)S(1)}, f32[2,256,256]{2,1,0:T(8,128)S(1)}, u32[]{:S(2)}, u32[]{:S(2)}) collective-permute-start(f32[2,256,256]{2,1,0:T(8,128)S(1)} %get-tuple-element.38), channel_id=1, source_target_pairs={{0,1},{1,2},{2,3},{3,4},{4,5},{5,6},{6,7},{7,8},{8,9},{9,10},{10,1... | collective-permute-start | bytes 1572872 | tf_op jit(solution)/shard_map/ppermute | solution.py:91
  410.4 11.8 %collective-permute-start.24 = (f32[2,256,256]{2,1,0:T(8,128)S(1)}, f32[2,256,256]{2,1,0:T(8,128)S(1)}, u32[]{:S(2)}, u32[]{:S(2)}) collective-permute-start(f32[2,256,256]{2,1,0:T(8,128)S(1)} %get-tuple-element.40), channel_id=1, source_target_pairs={{0,8},{1,9},{2,10},{3,11},{4,12},{5,13},{6,14},{7,15},{8,16},{9,17... | collective-permute-start | bytes 1572872 | tf_op jit(solution)/shard_map/ppermute | solution.py:91
  412.0 21.4 %collective-permute-start.25 = (f32[2,256,256]{2,1,0:T(8,128)S(1)}, f32[2,256,256]{2,1,0:T(8,128)S(1)}, u32[]{:S(2)}, u32[]{:S(2)}) collective-permute-start(f32[2,256,256]{2,1,0:T(8,128)S(1)} %get-tuple-element.39), channel_id=1, source_target_pairs={{0,9},{1,10},{2,11},{3,12},{4,13},{5,14},{6,15},{7,16},{8,17},{9,1... | collective-permute-start | bytes 1572872 | tf_op jit(solution)/shard_map/ppermute | solution.py:91
  433.7 3.1 collective-permute-start.26
  436.8 7.6 %collective-permute-start.27 = (f32[2,128,256]{2,1,0:T(8,128)S(1)}, f32[2,128,256]{2,1,0:T(8,128)S(1)}, u32[]{:S(2)}, u32[]{:S(2)}) collective-permute-start(f32[2,128,256]{2,1,0:T(8,128)S(1)} %dynamic-slice_add_fusion), channel_id=1, source_target_pairs={{0,64},{32,96},{64,0},{96,32},{128,192},{160,224},{192,128},{224,1... | collective-permute-start | bytes 786440 | tf_op jit(solution)/shard_map/ppermute | solution.py:95
  444.4 14.8 %collective-permute-start.28 = (f32[2,128,256]{2,1,0:T(8,128)S(1)}, f32[2,128,256]{2,1,0:T(8,128)S(1)}, u32[]{:S(2)}, u32[]{:S(2)}) collective-permute-start(f32[2,128,256]{2,1,0:T(8,128)S(1)} %add.384), channel_id=1, source_target_pairs={{0,128},{32,160},{64,192},{96,224},{128,0},{160,32},{192,64},{224,... | collective-permute-start | bytes 786440 | tf_op jit(solution)/shard_map/ppermute | solution.py:95
  459.3 1.7 collective-permute-start.29
  (30 other events, 365.2 us)

commit v4 on v3

--- a/solution.py
+++ b/solution.py
@@ -85,10 +85,21 @@
     return jnp.max(gathered)
 
 
-def from_offset(block, axis, distance):
-    devices = range(lax.axis_size(axis))
-    route = [(i + distance, i) for i in devices if i + distance in devices]
-    return lax.ppermute(block, axis, route)
+def from_tile(block, rows, columns):
+    waves, tiles = lax.axis_size("wave"), lax.axis_size("tile")
+    grid_rows = tiles // GRID_X
+    half = GRID_X // 2
+    pairs = []
+    for target in range(tiles):
+        row, col = target // GRID_X + rows, target % GRID_X + columns
+        if not (0 <= row < grid_rows and 0 <= col < GRID_X):
+            continue
+        source = row * GRID_X + col
+        crossing = (col // half) != ((target % GRID_X) // half)
+        for wave in range(waves):
+            giver = (waves // 2 - 1 - wave // 2) * 2 + wave % 2 if crossing else wave
+            pairs.append((giver * tiles + source, wave * tiles + target))
+    return lax.ppermute(block, ("wave", "tile"), pairs)
 
 
 def partner(block, bit):
@@ -123,14 +134,11 @@
     tile_height, tile_width = tile_now.shape
     window = illumination.shape[-1]
     slots = live_slots.shape[2]
-    column = lax.axis_index("tile") % GRID_X
-    keep_right = (column != GRID_X - 1).astype(jnp.float32)
-    keep_left = (column != 0).astype(jnp.float32)
     cos_table, sin_table = tables(window)
     exact = lax.Precision.HIGHEST
-    right = from_offset(tile_now, "tile", 1) * keep_right
-    below = from_offset(tile_now, "tile", GRID_X)
-    corner = from_offset(tile_now, "tile", GRID_X + 1) * keep_right
+    right = from_tile(tile_now, 0, 1)
+    below = from_tile(tile_now, 1, 0)
+    corner = from_tile(tile_now, 1, 1)
     extended = jnp.concatenate(
         [jnp.concatenate([tile_now, right], 1), jnp.concatenate([below, corner], 1)], 0
     )
@@ -150,16 +158,16 @@
         placed_rows = jnp.einsum("sij,smjk->smik", row_pick, wins, precision=exact)
         spread = jnp.einsum("smik,slk->mil", placed_rows, col_pick, precision=exact)
         own = spread[:, :tile_height, :tile_width]
-        from_left = from_offset(spread[:, :tile_height, tile_width:], "tile", -1) * keep_left
-        from_above = from_offset(spread[:, tile_height:, :tile_width], "tile", -GRID_X)
+        from_left = from_tile(spread[:, :tile_height, tile_width:], 0, -1)
+        from_above = from_tile(spread[:, tile_height:, :tile_width], -1, 0)
         from_corner = (
-            from_offset(spread[:, tile_height:, tile_width:], "tile", -GRID_X - 1) * keep_left
+            from_tile(spread[:, tile_height:, tile_width:], -1, -1)
         )
         maps = wave_sum(own + from_left + from_above + from_corner)
         if batch_index + 1 < BATCHES:
-            maps_right = from_offset(maps, "tile", 1) * keep_right
-            maps_below = from_offset(maps, "tile", GRID_X)
-            maps_corner = from_offset(maps, "tile", GRID_X + 1) * keep_right
+            maps_right = from_tile(maps, 0, 1)
+            maps_below = from_tile(maps, 1, 0)
+            maps_corner = from_tile(maps, 1, 1)
             maps = jnp.concatenate(
                 [
                     jnp.concatenate([maps, maps_right], 2),

time: 518 us -> 445 us (0.86)
  waiting for transfers between devices: 184 us -> 133 us
  starting transfers between devices: 150 us -> 137 us
    all_to_all x2, waiting for transfers between devices: 51.1 us -> 12.6 us  [tile_max(): gathered = lax.all_to_all(spread, 'tile', 0, 0, tiled=True)]
    all_to_all x2, starting transfers between devices: 97.5 us -> 77.7 us  [tile_max(): gathered = lax.all_to_all(spread, 'tile', 0, 0, tiled=True)]
    ppermute x18, waiting for transfers between devices: 63 us -> 53.3 us  [from_tile(): return lax.ppermute(block, ('wave', 'tile'), pairs)]
    ppermute x12, starting transfers between devices: 12.8 us -> 20.7 us  [partner(): lax.ppermute(block, 'wave', [(i, i ^ bit) for i in range(lax.axis_size('w...]
    mul x6 -> x0, other arithmetic: 6.26 us -> none  [the longest x2 2.16 us: shards(): maps_right = from_offset(maps, 'tile', 1) * keep_right]
  transfers between devices with their start and end apart: 32 -> 32, of which waited for: 25 -> 24; matrix products, arithmetic and copies ran while one was open for 7% -> 6% of each run, Pallas kernels for 0% -> 0%
where the time goes in v4:
time: 445 us; the launch traced here: 439 us
  starting transfers between devices  137 us (31%)
  waiting for transfers between devices  133 us (30%)
  other arithmetic  62 us (14%)
  blocking collectives  42.3 us (10%)
  matrix products  30.8 us (7%)
  local copies, waits for them, and re-layouts  30.7 us (7%)
    all_to_all x2, starting transfers between devices, tile_max(): gathered = lax.all_to_all(spread, 'tile', 0, 0, tiled=True)  77.7 us
    ppermute x12, waiting for transfers between devices, partner(): lax.ppermute(block, 'wave', [(i, i ^ bit) for i in range(lax.axis_size('w...  67.5 us
    ppermute x18, waiting for transfers between devices, from_tile(): return lax.ppermute(block, ('wave', 'tile'), pairs)  53.3 us
    all_to_all x1, blocking collectives, tile_max(): gathered = lax.all_to_all(spread, 'tile', 0, 0, tiled=True)  42.3 us
    ppermute x18, starting transfers between devices, from_tile(): return lax.ppermute(block, ('wave', 'tile'), pairs)  38.5 us
    ppermute x12, starting transfers between devices, partner(): lax.ppermute(block, 'wave', [(i, i ^ bit) for i in range(lax.axis_size('w...  20.7 us
    reduce_sum x3, other arithmetic, window_terms(): jnp.sum(slope_real * change_real + slope_imag * change_imag, axis=1)  17.9 us
    convert_element_type x3, other arithmetic, window_terms(): wave_real.astype(jnp.bfloat16)  13.9 us
  transfers between devices with their start and end apart: 32, of which 24 were waited for; matrix products, arithmetic and copies ran while one was open for 6% of the time, Pallas kernels for 0%

profile of v4, /device:TPU:1, one launch (start us, length us, event | category | flops | bytes accessed | tf_op | source)
XLA Modules:
  0.0 439.1 jit_solution(10759460686975171697)
XLA Ops:
  19.7 5.0 %fusion.205 = (bf16[2,2,256,256]{3,2,1,0:T(8,128)(2,1)S(1)}, bf16[2,2,256,256]{3,2,1,0:T(8,128)(2,1)S(1)}) fusion(f32[2,256,256]{2,1,0:T(8,128)S(1)} %get-tuple-element.54, f32[2]{0:T(128)S(1)} %copy-done.10, f32[2,256,256]{2,1,0:T(8,128)S(1)} %fusion.126, f32[2]{0:T(128)S(1)} %neg.15, f32[2,256,256]{2,1,0:T(8,128)S(1)} %get-tuple-element.53), kind=kLoop, calls=%fused_computation.319 | loop fusion | flops 3145728 | bytes 2621456 | tf_op jit(solution)/shard_map/convert_element_type | solution.py:58
  28.7 6.0 %fusion.52 = (f32[2,256,256]{2,1,0:T(8,128)}, f32[2,256,256]{2,1,0:T(8,128)}) fusion(f32[2,2,512,512]{3,2,1,0:T(8,128)S(1)} %fusion.69, f32[2]{0:T(128)S(1)} %copy-done.10, f32[2]{0:T(128)S(1)} %neg.15, f32[2,256,256]{2,1,0:T(8,128)S(1)} %get-tuple-element.54, f32[2,256,256]{2,1,0:T(8,128)S(1)} %fusion.126, f32[2,256,256]{2,1,0:T(8,128)S(1)} %get-tuple-element.53), kind=kLoop, calls=%fused_computation.87 | loop fusion | flops 7077888 | bytes 6815760 | tf_op jit(solution)/shard_map/reduce_sum | solution.py:76
  41.1 3.6 fusion.6
  47.2 5.5 %collective-permute-start.3 = (f32[2,256,256]{2,1,0:T(8,128)}, f32[2,256,256]{2,1,0:T(8,128)S(1)}, u32[]{:S(2)}, u32[]{:S(2)}) collective-permute-start(f32[2,256,256]{2,1,0:T(8,128)} %get-tuple-element.44), channel_id=1, source_target_pairs={{0,1},{32,33},{64,65},{96,97},{128,129},{160,161},{192,193},{224,2... | collective-permute-start | bytes 1572872 | tf_op jit(solution)/shard_map/ppermute | solution.py:102
  52.7 3.9 collective-permute-start.4
  56.7 4.1 collective-permute-start.5
  65.4 11.2 %collective-permute-done.5 = f32[2,256,256]{2,1,0:T(8,128)} collective-permute-done((f32[2,256,256]{2,1,0:T(8,128)}, f32[2,256,256]{2,1,0:T(8,128)}, u32[]{:S(2)}, u32[]{:S(2)}) %collective-permute-start.5) | collective-permute-done | bytes 524320 | tf_op jit(solution)/shard_map/ppermute | solution.py:102
  79.0 3.1 collective-permute-start.6
  86.3 6.2 %collective-permute-done.7 = f32[2,128,256]{2,1,0:T(8,128)S(1)} collective-permute-done((f32[2,128,256]{2,1,0:T(8,128)S(1)}, f32[2,128,256]{2,1,0:T(8,128)S(1)}, u32[]{:S(2)}, u32[]{:S(2)}) %collective-permute-start.7) | collective-permute-done | bytes 262176 | tf_op jit(solution)/shard_map/ppermute | solution.py:106
  92.5 3.1 collective-permute-start.8
  95.6 11.4 %collective-permute-done.8 = f32[2,128,256]{2,1,0:T(8,128)S(1)} collective-permute-done((f32[2,128,256]{2,1,0:T(8,128)S(1)}, f32[2,128,256]{2,1,0:T(8,128)S(1)}, u32[]{:S(2)}, u32[]{:S(2)}) %collective-permute-start.8) | collective-permute-done | bytes 262176 | tf_op jit(solution)/shard_map/ppermute | solution.py:106
  119.6 41.5 %all-to-all-start = ((f32[32,1,128]{2,1,0:T(1,128)}), f32[32,1,128]{2,1,0:T(1,128)}, u32[]{:S(2)}, u32[]{:S(2)}) async-start(f32[32,1,128]{2,1,0:T(1,128)} %broadcast_in_dim.8), calls=%async_computation | async-start | bytes 32768 | tf_op jit(solution)/shard_map/all_to_all | solution.py:84
  165.3 6.5 %all-to-all-done = f32[32,1,128]{2,1,0:T(1,128)} async-done(((f32[32,1,128]{2,1,0:T(1,128)}), f32[32,1,128]{2,1,0:T(1,128)}, u32[]{:S(2)}, u32[]{:S(2)}) %all-to-all-start) | async-done | bytes 16416 | tf_op jit(solution)/shard_map/all_to_all | solution.py:84
  179.0 4.5 %fusion.207 = (bf16[2,2,256,256]{3,2,1,0:T(8,128)(2,1)S(1)}, bf16[2,2,256,256]{3,2,1,0:T(8,128)(2,1)S(1)}) fusion(f32[2,256,256]{2,1,0:T(8,128)S(1)} %get-tuple-element.54, f32[2]{0:T(128)S(1)} %copy-done.10, f32[2,256,256]{2,1,0:T(8,128)S(1)} %fusion.123, f32[2]{0:T(128)S(1)} %neg.15, f32[2,256,256]{2,1,0:T(8,128)S(1)} %get-tuple-element.53), kind=kLoop, calls=%fused_computation.321 | loop fusion | flops 3145728 | bytes 2621456 | tf_op jit(solution)/shard_map/convert_element_type | solution.py:58
  187.8 6.0 %fusion.38 = (f32[2,256,256]{2,1,0:T(8,128)}, f32[2,256,256]{2,1,0:T(8,128)}) fusion(f32[2,2,512,512]{3,2,1,0:T(8,128)S(1)} %fusion.87, f32[2]{0:T(128)S(1)} %copy-done.10, f32[2]{0:T(128)S(1)} %neg.15, f32[2,256,256]{2,1,0:T(8,128)S(1)} %get-tuple-element.54, f32[2,256,256]{2,1,0:T(8,128)S(1)} %fusion.123, f32[2,256,256]{2,1,0:T(8,128)S(1)} %get-tuple-element.53), kind=kLoop, calls=%fused_computation.63 | loop fusion | flops 7077888 | bytes 6815760 | tf_op jit(solution)/shard_map/reduce_sum | solution.py:76
  199.5 3.6 fusion.9
  209.9 4.7 %collective-permute-done.13 = f32[2,256,256]{2,1,0:T(8,128)S(1)} collective-permute-done((f32[2,256,256]{2,1,0:T(8,128)S(1)}, f32[2,256,256]{2,1,0:T(8,128)S(1)}, u32[]{:S(2)}, u32[]{:S(2)}) %collective-permute-start.13) | collective-permute-done | bytes 524320 | tf_op jit(solution)/shard_map/ppermute | solution.py:102
  216.1 11.2 %collective-permute-done.15 = f32[2,256,256]{2,1,0:T(8,128)S(1)} collective-permute-done((f32[2,256,256]{2,1,0:T(8,128)S(1)}, f32[2,256,256]{2,1,0:T(8,128)S(1)}, u32[]{:S(2)}, u32[]{:S(2)}) %collective-permute-start.15) | collective-permute-done | bytes 524320 | tf_op jit(solution)/shard_map/ppermute | solution.py:102
  227.5 3.8 collective-permute-start.16
  232.7 7.5 %collective-permute-done.17 = f32[2,128,256]{2,1,0:T(8,128)S(1)} collective-permute-done((f32[2,128,256]{2,1,0:T(8,128)S(1)}, f32[2,128,256]{2,1,0:T(8,128)S(1)}, u32[]{:S(2)}, u32[]{:S(2)}) %collective-permute-start.17) | collective-permute-done | bytes 262176 | tf_op jit(solution)/shard_map/ppermute | solution.py:106
  240.4 14.6 %collective-permute-done.18 = f32[2,128,256]{2,1,0:T(8,128)S(1)} collective-permute-done((f32[2,128,256]{2,1,0:T(8,128)S(1)}, f32[2,128,256]{2,1,0:T(8,128)S(1)}, u32[]{:S(2)}, u32[]{:S(2)}) %collective-permute-start.18) | collective-permute-done | bytes 262176 | tf_op jit(solution)/shard_map/ppermute | solution.py:106
  264.7 36.2 %all-to-all-start.1 = ((f32[32,1,128]{2,1,0:T(1,128)}), f32[32,1,128]{2,1,0:T(1,128)S(1)}, u32[]{:S(2)}, u32[]{:S(2)}) async-start(f32[32,1,128]{2,1,0:T(1,128)} %broadcast_in_dim.9), calls=%async_computation.1 | async-start | bytes 32768 | tf_op jit(solution)/shard_map/all_to_all | solution.py:84
  305.8 6.1 %all-to-all-done.1 = f32[32,1,128]{2,1,0:T(1,128)S(1)} async-done(((f32[32,1,128]{2,1,0:T(1,128)}), f32[32,1,128]{2,1,0:T(1,128)S(1)}, u32[]{:S(2)}, u32[]{:S(2)}) %all-to-all-start.1) | async-done | bytes 16416 | tf_op jit(solution)/shard_map/all_to_all | solution.py:84
  317.6 4.5 %fusion.209 = (bf16[2,2,256,256]{3,2,1,0:T(8,128)(2,1)S(1)}, bf16[2,2,256,256]{3,2,1,0:T(8,128)(2,1)S(1)}) fusion(f32[2,256,256]{2,1,0:T(8,128)S(1)} %get-tuple-element.54, f32[2]{0:T(128)S(1)} %copy-done.11, f32[2,256,256]{2,1,0:T(8,128)S(1)} %fusion.120, f32[2]{0:T(128)S(1)} %copy-done.13, f32[2,256,256]{2,1,0:T(8,128)S(1)} %get-tuple-element.53), kind=kLoop, calls=%fused_computation.323 | loop fusion | flops 3145728 | bytes 2621456 | tf_op jit(solution)/shard_map/convert_element_type | solution.py:58
  326.3 5.8 %fusion.24 = (f32[2,256,256]{2,1,0:T(8,128)}, f32[2,256,256]{2,1,0:T(8,128)S(1)}) fusion(f32[2,2,512,512]{3,2,1,0:T(8,128)S(1)} %fusion.105, f32[2]{0:T(128)S(1)} %copy-done.11, f32[2]{0:T(128)S(1)} %copy-done.13, f32[2,256,256]{2,1,0:T(8,128)S(1)} %get-tuple-element.54, f32[2,256,256]{2,1,0:T(8,128)S(1)} %fusion.120, f32[2,256,256]{2,1,0:T(8,128)S(1)} %get-tuple-element.53), kind=kLoop, calls=%fused_computation.39 | loop fusion | flops 7077888 | bytes 6815760 | tf_op jit(solution)/shard_map/reduce_sum | solution.py:76
  335.0 3.6 fusion.12
  345.3 4.3 collective-permute-done.23
  351.5 11.2 %collective-permute-done.25 = f32[2,256,256]{2,1,0:T(8,128)S(1)} collective-permute-done((f32[2,256,256]{2,1,0:T(8,128)S(1)}, f32[2,256,256]{2,1,0:T(8,128)S(1)}, u32[]{:S(2)}, u32[]{:S(2)}) %collective-permute-start.25) | collective-permute-done | bytes 524320 | tf_op jit(solution)/shard_map/ppermute | solution.py:102
  363.0 3.9 collective-permute-start.26
  368.1 7.5 %collective-permute-done.27 = f32[2,128,256]{2,1,0:T(8,128)S(1)} collective-permute-done((f32[2,128,256]{2,1,0:T(8,128)S(1)}, f32[2,128,256]{2,1,0:T(8,128)S(1)}, u32[]{:S(2)}, u32[]{:S(2)}) %collective-permute-start.27) | collective-permute-done | bytes 262176 | tf_op jit(solution)/shard_map/ppermute | solution.py:106
  377.4 12.9 %collective-permute-done.28 = f32[2,128,256]{2,1,0:T(8,128)S(1)} collective-permute-done((f32[2,128,256]{2,1,0:T(8,128)S(1)}, f32[2,128,256]{2,1,0:T(8,128)S(1)}, u32[]{:S(2)}, u32[]{:S(2)}) %collective-permute-start.28) | collective-permute-done | bytes 262176 | tf_op jit(solution)/shard_map/ppermute | solution.py:106
  393.6 42.3 %all_to_all.18 = f32[32,1,128]{2,1,0:T(1,128)S(1)} all-to-all(f32[32,1,128]{2,1,0:T(1,128)S(1)} %broadcast_in_dim.10), channel_id=1, replica_groups=mesh['wave'=8,'tile'=32] {'tile'}, dimensions={0} | all-to-all | bytes 32768 | tf_op jit(solution)/shard_map/all_to_all | solution.py:84
  (186 shorter events, 130.8 us)
Async XLA Ops:
  0.0 13.9 %collective-permute-start = (f32[256,256]{1,0:T(8,128)}, f32[256,256]{1,0:T(8,128)}, u32[]{:S(2)}, u32[]{:S(2)}) collective-permute-start(f32[256,256]{1,0:T(8,128)} %bitcast.147), channel_id=1, source_target_pairs={{1,0},{33,32},{65,64},{97,96},{129,128},{161,160},{193,192},{225,2... | collective-permute-start | bytes 786440 | tf_op jit(solution)/shard_map/ppermute | solution.py:102
  1.4 12.5 %collective-permute-start.1 = (f32[256,256]{1,0:T(8,128)}, f32[256,256]{1,0:T(8,128)}, u32[]{:S(2)}, u32[]{:S(2)}) collective-permute-start(f32[256,256]{1,0:T(8,128)} %bitcast.148), channel_id=1, source_target_pairs={{8,0},{40,32},{72,64},{104,96},{136,128},{168,160},{200,192},{232,... | collective-permute-start | bytes 786440 | tf_op jit(solution)/shard_map/ppermute | solution.py:102
  2.7 13.7 %collective-permute-start.2 = (f32[256,256]{1,0:T(8,128)}, f32[256,256]{1,0:T(8,128)}, u32[]{:S(2)}, u32[]{:S(2)}) collective-permute-start(f32[256,256]{1,0:T(8,128)} %bitcast.149), channel_id=1, source_target_pairs={{9,0},{41,32},{73,64},{105,96},{137,128},{169,160},{201,192},{233,... | collective-permute-start | bytes 786440 | tf_op jit(solution)/shard_map/ppermute | solution.py:102
  47.2 15.3 %collective-permute-start.3 = (f32[2,256,256]{2,1,0:T(8,128)}, f32[2,256,256]{2,1,0:T(8,128)S(1)}, u32[]{:S(2)}, u32[]{:S(2)}) collective-permute-start(f32[2,256,256]{2,1,0:T(8,128)} %get-tuple-element.44), channel_id=1, source_target_pairs={{0,1},{32,33},{64,65},{96,97},{128,129},{160,161},{192,193},{224,2... | collective-permute-start | bytes 1572872 | tf_op jit(solution)/shard_map/ppermute | solution.py:102
  52.7 12.6 %collective-permute-start.4 = (f32[2,256,256]{2,1,0:T(8,128)}, f32[2,256,256]{2,1,0:T(8,128)}, u32[]{:S(2)}, u32[]{:S(2)}) collective-permute-start(f32[2,256,256]{2,1,0:T(8,128)} %get-tuple-element.46), channel_id=1, source_target_pairs={{0,8},{32,40},{64,72},{96,104},{128,136},{160,168},{192,200},{224,... | collective-permute-start | bytes 1572872 | tf_op jit(solution)/shard_map/ppermute | solution.py:102
  56.7 19.9 %collective-permute-start.5 = (f32[2,256,256]{2,1,0:T(8,128)}, f32[2,256,256]{2,1,0:T(8,128)}, u32[]{:S(2)}, u32[]{:S(2)}) collective-permute-start(f32[2,256,256]{2,1,0:T(8,128)} %get-tuple-element.45), channel_id=1, source_target_pairs={{0,9},{32,41},{64,73},{96,105},{128,137},{160,169},{192,201},{224,... | collective-permute-start | bytes 1572872 | tf_op jit(solution)/shard_map/ppermute | solution.py:102
  79.0 4.6 %collective-permute-start.6 = (f32[2,128,256]{2,1,0:T(8,128)}, f32[2,128,256]{2,1,0:T(8,128)}, u32[]{:S(2)}, u32[]{:S(2)}) collective-permute-start(f32[2,128,256]{2,1,0:T(8,128)} %constant_dynamic-slice_fusion.2), channel_id=1, source_target_pairs={{0,32},{32,0},{64,96},{96,64},{128,160},{160,128},{192,224},{224,1... | collective-permute-start | bytes 786440 | tf_op jit(solution)/shard_map/ppermute | solution.py:106
  84.6 7.9 %collective-permute-start.7 = (f32[2,128,256]{2,1,0:T(8,128)S(1)}, f32[2,128,256]{2,1,0:T(8,128)S(1)}, u32[]{:S(2)}, u32[]{:S(2)}) collective-permute-start(f32[2,128,256]{2,1,0:T(8,128)S(1)} %dynamic-slice_add_fusion.2), channel_id=1, source_target_pairs={{0,64},{32,96},{64,0},{96,32},{128,192},{160,224},{192,128},{224,1... | collective-permute-start | bytes 786440 | tf_op jit(solution)/shard_map/ppermute | solution.py:106
  92.5 14.5 %collective-permute-start.8 = (f32[2,128,256]{2,1,0:T(8,128)S(1)}, f32[2,128,256]{2,1,0:T(8,128)S(1)}, u32[]{:S(2)}, u32[]{:S(2)}) collective-permute-start(f32[2,128,256]{2,1,0:T(8,128)S(1)} %add.328), channel_id=1, source_target_pairs={{0,128},{32,160},{64,192},{96,224},{128,0},{160,32},{192,64},{224,... | collective-permute-start | bytes 786440 | tf_op jit(solution)/shard_map/ppermute | solution.py:106
  107.0 2.9 collective-permute-start.9
  111.8 62.0 %collective-permute-start.10 = (f32[2,256,256]{2,1,0:T(8,128)}, f32[2,256,256]{2,1,0:T(8,128)}, u32[]{:S(2)}, u32[]{:S(2)}) collective-permute-start(f32[2,256,256]{2,1,0:T(8,128)} %pad_maximum_fusion), channel_id=1, source_target_pairs={{1,0},{33,32},{65,64},{97,96},{129,128},{161,160},{193,192},{225,2... | collective-permute-start | bytes 1572872 | tf_op jit(solution)/shard_map/ppermute | solution.py:102
  113.1 60.8 %collective-permute-start.11 = (f32[2,256,256]{2,1,0:T(8,128)}, f32[2,256,256]{2,1,0:T(8,128)}, u32[]{:S(2)}, u32[]{:S(2)}) collective-permute-start(f32[2,256,256]{2,1,0:T(8,128)} %pad_maximum_fusion), channel_id=1, source_target_pairs={{8,0},{40,32},{72,64},{104,96},{136,128},{168,160},{200,192},{232,... | collective-permute-start | bytes 1572872 | tf_op jit(solution)/shard_map/ppermute | solution.py:102
  114.4 59.5 %collective-permute-start.12 = (f32[2,256,256]{2,1,0:T(8,128)}, f32[2,256,256]{2,1,0:T(8,128)}, u32[]{:S(2)}, u32[]{:S(2)}) collective-permute-start(f32[2,256,256]{2,1,0:T(8,128)} %pad_maximum_fusion), channel_id=1, source_target_pairs={{9,0},{41,32},{73,64},{105,96},{137,128},{169,160},{201,192},{233,... | collective-permute-start | bytes 1572872 | tf_op jit(solution)/shard_map/ppermute | solution.py:102
  119.6 52.3 %all-to-all-start = ((f32[32,1,128]{2,1,0:T(1,128)}), f32[32,1,128]{2,1,0:T(1,128)}, u32[]{:S(2)}, u32[]{:S(2)}) async-start(f32[32,1,128]{2,1,0:T(1,128)} %broadcast_in_dim.8), calls=%async_computation | async-start | bytes 32768 | tf_op jit(solution)/shard_map/all_to_all | solution.py:84
  203.2 11.3 %collective-permute-start.13 = (f32[2,256,256]{2,1,0:T(8,128)S(1)}, f32[2,256,256]{2,1,0:T(8,128)S(1)}, u32[]{:S(2)}, u32[]{:S(2)}) collective-permute-start(f32[2,256,256]{2,1,0:T(8,128)S(1)} %get-tuple-element.41), channel_id=1, source_target_pairs={{0,1},{32,33},{64,65},{96,97},{128,129},{160,161},{192,193},{224,2... | collective-permute-start | bytes 1572872 | tf_op jit(solution)/shard_map/ppermute | solution.py:102
  205.6 10.5 %collective-permute-start.14 = (f32[2,256,256]{2,1,0:T(8,128)S(1)}, f32[2,256,256]{2,1,0:T(8,128)S(1)}, u32[]{:S(2)}, u32[]{:S(2)}) collective-permute-start(f32[2,256,256]{2,1,0:T(8,128)S(1)} %get-tuple-element.43), channel_id=1, source_target_pairs={{0,8},{32,40},{64,72},{96,104},{128,136},{160,168},{192,200},{224,... | collective-permute-start | bytes 1572872 | tf_op jit(solution)/shard_map/ppermute | solution.py:102
  207.8 19.6 %collective-permute-start.15 = (f32[2,256,256]{2,1,0:T(8,128)S(1)}, f32[2,256,256]{2,1,0:T(8,128)S(1)}, u32[]{:S(2)}, u32[]{:S(2)}) collective-permute-start(f32[2,256,256]{2,1,0:T(8,128)S(1)} %get-tuple-element.42), channel_id=1, source_target_pairs={{0,9},{32,41},{64,73},{96,105},{128,137},{160,169},{192,201},{224,... | collective-permute-start | bytes 1572872 | tf_op jit(solution)/shard_map/ppermute | solution.py:102
  227.5 5.0 %collective-permute-start.16 = (f32[2,128,256]{2,1,0:T(8,128)S(1)}, f32[2,128,256]{2,1,0:T(8,128)S(1)}, u32[]{:S(2)}, u32[]{:S(2)}) collective-permute-start(f32[2,128,256]{2,1,0:T(8,128)S(1)} %constant_dynamic-slice_fusion.1), channel_id=1, source_target_pairs={{0,32},{32,0},{64,96},{96,64},{128,160},{160,128},{192,224},{224,1... | collective-permute-start | bytes 786440 | tf_op jit(solution)/shard_map/ppermute | solution.py:106
  232.6 7.6 %collective-permute-start.17 = (f32[2,128,256]{2,1,0:T(8,128)S(1)}, f32[2,128,256]{2,1,0:T(8,128)S(1)}, u32[]{:S(2)}, u32[]{:S(2)}) collective-permute-start(f32[2,128,256]{2,1,0:T(8,128)S(1)} %dynamic-slice_add_fusion.1), channel_id=1, source_target_pairs={{0,64},{32,96},{64,0},{96,32},{128,192},{160,224},{192,128},{224,1... | collective-permute-start | bytes 786440 | tf_op jit(solution)/shard_map/ppermute | solution.py:106
  240.2 14.8 %collective-permute-start.18 = (f32[2,128,256]{2,1,0:T(8,128)S(1)}, f32[2,128,256]{2,1,0:T(8,128)S(1)}, u32[]{:S(2)}, u32[]{:S(2)}) collective-permute-start(f32[2,128,256]{2,1,0:T(8,128)S(1)} %add.354), channel_id=1, source_target_pairs={{0,128},{32,160},{64,192},{96,224},{128,0},{160,32},{192,64},{224,... | collective-permute-start | bytes 786440 | tf_op jit(solution)/shard_map/ppermute | solution.py:106
  255.1 1.7 collective-permute-start.19
  257.7 55.5 %collective-permute-start.20 = (f32[2,256,256]{2,1,0:T(8,128)}, f32[2,256,256]{2,1,0:T(8,128)}, u32[]{:S(2)}, u32[]{:S(2)}) collective-permute-start(f32[2,256,256]{2,1,0:T(8,128)} %pad_maximum_fusion.1), channel_id=1, source_target_pairs={{1,0},{33,32},{65,64},{97,96},{129,128},{161,160},{193,192},{225,2... | collective-permute-start | bytes 1572872 | tf_op jit(solution)/shard_map/ppermute | solution.py:102
  259.0 54.2 %collective-permute-start.21 = (f32[2,256,256]{2,1,0:T(8,128)}, f32[2,256,256]{2,1,0:T(8,128)}, u32[]{:S(2)}, u32[]{:S(2)}) collective-permute-start(f32[2,256,256]{2,1,0:T(8,128)} %pad_maximum_fusion.1), channel_id=1, source_target_pairs={{8,0},{40,32},{72,64},{104,96},{136,128},{168,160},{200,192},{232,... | collective-permute-start | bytes 1572872 | tf_op jit(solution)/shard_map/ppermute | solution.py:102
  260.3 53.0 %collective-permute-start.22 = (f32[2,256,256]{2,1,0:T(8,128)}, f32[2,256,256]{2,1,0:T(8,128)}, u32[]{:S(2)}, u32[]{:S(2)}) collective-permute-start(f32[2,256,256]{2,1,0:T(8,128)} %pad_maximum_fusion.1), channel_id=1, source_target_pairs={{9,0},{41,32},{73,64},{105,96},{137,128},{169,160},{201,192},{233,... | collective-permute-start | bytes 1572872 | tf_op jit(solution)/shard_map/ppermute | solution.py:102
  264.7 47.3 %all-to-all-start.1 = ((f32[32,1,128]{2,1,0:T(1,128)}), f32[32,1,128]{2,1,0:T(1,128)S(1)}, u32[]{:S(2)}, u32[]{:S(2)}) async-start(f32[32,1,128]{2,1,0:T(1,128)} %broadcast_in_dim.9), calls=%async_computation.1 | async-start | bytes 32768 | tf_op jit(solution)/shard_map/all_to_all | solution.py:84
  338.7 10.8 %collective-permute-start.23 = (f32[2,256,256]{2,1,0:T(8,128)S(1)}, f32[2,256,256]{2,1,0:T(8,128)S(1)}, u32[]{:S(2)}, u32[]{:S(2)}) collective-permute-start(f32[2,256,256]{2,1,0:T(8,128)S(1)} %get-tuple-element.38), channel_id=1, source_target_pairs={{0,1},{32,33},{64,65},{96,97},{128,129},{160,161},{192,193},{224,2... | collective-permute-start | bytes 1572872 | tf_op jit(solution)/shard_map/ppermute | solution.py:102
  340.9 10.6 %collective-permute-start.24 = (f32[2,256,256]{2,1,0:T(8,128)S(1)}, f32[2,256,256]{2,1,0:T(8,128)S(1)}, u32[]{:S(2)}, u32[]{:S(2)}) collective-permute-start(f32[2,256,256]{2,1,0:T(8,128)S(1)} %get-tuple-element.40), channel_id=1, source_target_pairs={{0,8},{32,40},{64,72},{96,104},{128,136},{160,168},{192,200},{224,... | collective-permute-start | bytes 1572872 | tf_op jit(solution)/shard_map/ppermute | solution.py:102
  343.2 19.5 %collective-permute-start.25 = (f32[2,256,256]{2,1,0:T(8,128)S(1)}, f32[2,256,256]{2,1,0:T(8,128)S(1)}, u32[]{:S(2)}, u32[]{:S(2)}) collective-permute-start(f32[2,256,256]{2,1,0:T(8,128)S(1)} %get-tuple-element.39), channel_id=1, source_target_pairs={{0,9},{32,41},{64,73},{96,105},{128,137},{160,169},{192,201},{224,... | collective-permute-start | bytes 1572872 | tf_op jit(solution)/shard_map/ppermute | solution.py:102
  363.0 5.0 %collective-permute-start.26 = (f32[2,128,256]{2,1,0:T(8,128)S(1)}, f32[2,128,256]{2,1,0:T(8,128)S(1)}, u32[]{:S(2)}, u32[]{:S(2)}) collective-permute-start(f32[2,128,256]{2,1,0:T(8,128)S(1)} %constant_dynamic-slice_fusion), channel_id=1, source_target_pairs={{0,32},{32,0},{64,96},{96,64},{128,160},{160,128},{192,224},{224,1... | collective-permute-start | bytes 786440 | tf_op jit(solution)/shard_map/ppermute | solution.py:106
  368.0 7.6 %collective-permute-start.27 = (f32[2,128,256]{2,1,0:T(8,128)S(1)}, f32[2,128,256]{2,1,0:T(8,128)S(1)}, u32[]{:S(2)}, u32[]{:S(2)}) collective-permute-start(f32[2,128,256]{2,1,0:T(8,128)S(1)} %dynamic-slice_add_fusion), channel_id=1, source_target_pairs={{0,64},{32,96},{64,0},{96,32},{128,192},{160,224},{192,128},{224,1... | collective-permute-start | bytes 786440 | tf_op jit(solution)/shard_map/ppermute | solution.py:106
  375.6 14.6 %collective-permute-start.28 = (f32[2,128,256]{2,1,0:T(8,128)S(1)}, f32[2,128,256]{2,1,0:T(8,128)S(1)}, u32[]{:S(2)}, u32[]{:S(2)}) collective-permute-start(f32[2,128,256]{2,1,0:T(8,128)S(1)} %add.380), channel_id=1, source_target_pairs={{0,128},{32,160},{64,192},{96,224},{128,0},{160,32},{192,64},{224,... | collective-permute-start | bytes 786440 | tf_op jit(solution)/shard_map/ppermute | solution.py:106
  390.3 2.0 collective-permute-start.29
  (23 other events, 279.5 us)

commit v5 on v4

--- a/solution.py
+++ b/solution.py
@@ -136,13 +136,13 @@
     slots = live_slots.shape[2]
     cos_table, sin_table = tables(window)
     exact = lax.Precision.HIGHEST
-    right = from_tile(tile_now, 0, 1)
-    below = from_tile(tile_now, 1, 0)
-    corner = from_tile(tile_now, 1, 1)
-    extended = jnp.concatenate(
-        [jnp.concatenate([tile_now, right], 1), jnp.concatenate([below, corner], 1)], 0
-    )
     for batch_index in range(BATCHES):
+        right = from_tile(tile_now, 0, 1)
+        below = from_tile(tile_now, 1, 0)
+        corner = from_tile(tile_now, 1, 1)
+        extended = jnp.concatenate(
+            [jnp.concatenate([tile_now, right], 1), jnp.concatenate([below, corner], 1)], 0
+        )
         chosen = batch_order[0, batch_index * slots : (batch_index + 1) * slots]
         places = positions[0][chosen]
         measured = amplitudes[0][chosen]
@@ -164,23 +164,8 @@
             from_tile(spread[:, tile_height:, tile_width:], -1, -1)
         )
         maps = wave_sum(own + from_left + from_above + from_corner)
-        if batch_index + 1 < BATCHES:
-            maps_right = from_tile(maps, 0, 1)
-            maps_below = from_tile(maps, 1, 0)
-            maps_corner = from_tile(maps, 1, 1)
-            maps = jnp.concatenate(
-                [
-                    jnp.concatenate([maps, maps_right], 2),
-                    jnp.concatenate([maps_below, maps_corner], 2),
-                ],
-                1,
-            )
-        largest = tile_max(jnp.max(maps[1, :tile_height, :tile_width]))
-        if batch_index + 1 < BATCHES:
-            extended = extended + 0.5 * maps[0] / (0.75 * maps[1] + 0.25 * largest)
-            tile_now = extended[:tile_height, :tile_width]
-        else:
-            tile_now = tile_now + 0.5 * maps[0] / (0.75 * maps[1] + 0.25 * largest)
+        largest = tile_max(jnp.max(maps[1]))
+        tile_now = tile_now + 0.5 * maps[0] / (0.75 * maps[1] + 0.25 * largest)
     return tile_now[None]
 
 

time: 445 us -> 454 us (1.020)
  blocking collectives: 42.3 us -> 128 us
  starting transfers between devices: 137 us -> 58.5 us
  waiting for transfers between devices: 133 us -> 143 us
  local copies, waits for them, and re-layouts: 30.7 us -> 23.7 us
    all_to_all x1 -> x3, blocking collectives: 42.3 us -> 128 us  [tile_max(): gathered = lax.all_to_all(spread, 'tile', 0, 0, tiled=True)]
    all_to_all x2 -> x0, starting transfers between devices: 77.7 us -> none  [tile_max(): gathered = lax.all_to_all(spread, 'tile', 0, 0, tiled=True)]
    ppermute x18, waiting for transfers between devices: 53.3 us -> 73.1 us  [from_tile(): return lax.ppermute(block, ('wave', 'tile'), pairs)]
    all_to_all x2 -> x0, waiting for transfers between devices: 12.6 us -> none  [tile_max(): gathered = lax.all_to_all(spread, 'tile', 0, 0, tiled=True)]
    concatenate x4 -> x0, other arithmetic: 4.98 us -> none  [the longest x2 3.3 us: shards(): jnp.concatenate([jnp.concatenate([maps, maps_right], 2), jnp.concatenate(...]
  transfers between devices with their start and end apart: 32 -> 30, of which waited for: 24 -> 28; matrix products, arithmetic and copies ran while one was open for 6% -> 4% of each run, Pallas kernels for 0% -> 0%
where the time goes in v5:
time: 454 us; the launch traced here: 448 us
  waiting for transfers between devices  143 us (31%)
  blocking collectives  128 us (28%)
  starting transfers between devices  58.5 us (13%)
  other arithmetic  58.3 us (13%)
  matrix products  33.8 us (7%)
  local copies, waits for them, and re-layouts  23.7 us (5%)
    all_to_all x3, blocking collectives, tile_max(): gathered = lax.all_to_all(spread, 'tile', 0, 0, tiled=True)  128 us
    ppermute x18, waiting for transfers between devices, from_tile(): return lax.ppermute(block, ('wave', 'tile'), pairs)  73.1 us
    ppermute x12, waiting for transfers between devices, partner(): lax.ppermute(block, 'wave', [(i, i ^ bit) for i in range(lax.axis_size('w...  69.4 us
    ppermute x18, starting transfers between devices, from_tile(): return lax.ppermute(block, ('wave', 'tile'), pairs)  40.2 us
    ppermute x12, starting transfers between devices, partner(): lax.ppermute(block, 'wave', [(i, i ^ bit) for i in range(lax.axis_size('w...  18.3 us
    reduce_sum x3, other arithmetic, window_terms(): jnp.sum(slope_real * change_real + slope_imag * change_imag, axis=1)  17.9 us
    convert_element_type x3, other arithmetic, window_terms(): wave_real.astype(jnp.bfloat16)  13.6 us
    dot_general x3, matrix products, shards(): spread = jnp.einsum('smik,slk->mil', placed_rows, col_pick, precision=exact)  10.7 us
  transfers between devices with their start and end apart: 30, of which 28 were waited for; matrix products, arithmetic and copies ran while one was open for 4% of the time, Pallas kernels for 0%

profile of v5, /device:TPU:1, one launch (start us, length us, event | category | flops | bytes accessed | tf_op | source)
XLA Modules:
  0.0 447.9 jit_solution(14895399331526336866)
XLA Ops:
  19.7 4.6 %fusion.216 = (bf16[2,2,256,256]{3,2,1,0:T(8,128)(2,1)S(1)}, bf16[2,2,256,256]{3,2,1,0:T(8,128)(2,1)S(1)}) fusion(f32[2,256,256]{2,1,0:T(8,128)S(1)} %get-tuple-element.58, f32[2]{0:T(128)S(1)} %copy-done.9, f32[2,256,256]{2,1,0:T(8,128)S(1)} %fusion.133, f32[2]{0:T(128)S(1)} %neg.15, f32[2,256,256]{2,1,0:T(8,128)S(1)} %get-tuple-element.57), kind=kLoop, calls=%fused_computation.328 | loop fusion | flops 3145728 | bytes 2621456 | tf_op jit(solution)/shard_map/convert_element_type | solution.py:58
  28.3 6.0 %fusion.44 = (f32[2,256,256]{2,1,0:T(8,128)}, f32[2,256,256]{2,1,0:T(8,128)}) fusion(f32[2,2,512,512]{3,2,1,0:T(8,128)S(1)} %fusion.68, f32[2]{0:T(128)S(1)} %copy-done.9, f32[2]{0:T(128)S(1)} %neg.15, f32[2,256,256]{2,1,0:T(8,128)S(1)} %get-tuple-element.58, f32[2,256,256]{2,1,0:T(8,128)S(1)} %fusion.133, f32[2,256,256]{2,1,0:T(8,128)S(1)} %get-tuple-element.57), kind=kLoop, calls=%fused_computation.73 | loop fusion | flops 7077888 | bytes 6815760 | tf_op jit(solution)/shard_map/reduce_sum | solution.py:76
  40.7 3.6 fusion.6
  46.8 5.5 %collective-permute-start.3 = (f32[2,256,256]{2,1,0:T(8,128)}, f32[2,256,256]{2,1,0:T(8,128)S(1)}, u32[]{:S(2)}, u32[]{:S(2)}) collective-permute-start(f32[2,256,256]{2,1,0:T(8,128)} %get-tuple-element.48), channel_id=1, source_target_pairs={{0,1},{32,33},{64,65},{96,97},{128,129},{160,161},{192,193},{224,2... | collective-permute-start | bytes 1572872 | tf_op jit(solution)/shard_map/ppermute | solution.py:102
  52.4 3.9 collective-permute-start.4
  56.3 4.1 collective-permute-start.5
  65.0 11.2 %collective-permute-done.5 = f32[2,256,256]{2,1,0:T(8,128)} collective-permute-done((f32[2,256,256]{2,1,0:T(8,128)}, f32[2,256,256]{2,1,0:T(8,128)}, u32[]{:S(2)}, u32[]{:S(2)}) %collective-permute-start.5) | collective-permute-done | bytes 524320 | tf_op jit(solution)/shard_map/ppermute | solution.py:102
  86.1 6.2 %collective-permute-done.7 = f32[2,128,256]{2,1,0:T(8,128)S(1)} collective-permute-done((f32[2,128,256]{2,1,0:T(8,128)S(1)}, f32[2,128,256]{2,1,0:T(8,128)S(1)}, u32[]{:S(2)}, u32[]{:S(2)}) %collective-permute-start.7) | collective-permute-done | bytes 262176 | tf_op jit(solution)/shard_map/ppermute | solution.py:106
  95.5 11.4 %collective-permute-done.8 = f32[2,128,256]{2,1,0:T(8,128)S(1)} collective-permute-done((f32[2,128,256]{2,1,0:T(8,128)S(1)}, f32[2,128,256]{2,1,0:T(8,128)S(1)}, u32[]{:S(2)}, u32[]{:S(2)}) %collective-permute-start.8) | collective-permute-done | bytes 262176 | tf_op jit(solution)/shard_map/ppermute | solution.py:106
  112.2 46.7 %all_to_all.18 = f32[32,1,128]{2,1,0:T(1,128)} all-to-all(f32[32,1,128]{2,1,0:T(1,128)S(1)} %broadcast_in_dim.6), channel_id=1, replica_groups=mesh['wave'=8,'tile'=32] {'tile'}, dimensions={0} | all-to-all | bytes 32768 | tf_op jit(solution)/shard_map/all_to_all | solution.py:84
  172.4 7.1 %collective-permute-done.12 = f32[256,256]{1,0:T(8,128)} collective-permute-done((f32[256,256]{1,0:T(8,128)}, f32[256,256]{1,0:T(8,128)}, u32[]{:S(2)}, u32[]{:S(2)}) %collective-permute-start.12) | collective-permute-done | bytes 262176 | tf_op jit(solution)/shard_map/ppermute | solution.py:102
  182.7 4.5 fusion.218
  191.4 6.0 %fusion.34 = (f32[2,256,256]{2,1,0:T(8,128)}, f32[2,256,256]{2,1,0:T(8,128)}) fusion(f32[2,2,512,512]{3,2,1,0:T(8,128)S(1)} %fusion.93, f32[2]{0:T(128)S(1)} %copy-done.9, f32[2]{0:T(128)S(1)} %neg.15, f32[2,256,256]{2,1,0:T(8,128)S(1)} %get-tuple-element.58, f32[2,256,256]{2,1,0:T(8,128)S(1)} %fusion.130, f32[2,256,256]{2,1,0:T(8,128)S(1)} %get-tuple-element.57), kind=kLoop, calls=%fused_computation.55 | loop fusion | flops 7077888 | bytes 6815760 | tf_op jit(solution)/shard_map/reduce_sum | solution.py:76
  203.8 3.6 fusion.9
  209.3 3.4 collective-permute-start.14
  217.4 4.2 collective-permute-done.14
  221.5 11.2 %collective-permute-done.15 = f32[2,256,256]{2,1,0:T(8,128)S(1)} collective-permute-done((f32[2,256,256]{2,1,0:T(8,128)S(1)}, f32[2,256,256]{2,1,0:T(8,128)S(1)}, u32[]{:S(2)}, u32[]{:S(2)}) %collective-permute-start.15) | collective-permute-done | bytes 524320 | tf_op jit(solution)/shard_map/ppermute | solution.py:102
  233.0 3.5 collective-permute-start.16
  237.8 7.5 %collective-permute-done.17 = f32[2,128,256]{2,1,0:T(8,128)S(1)} collective-permute-done((f32[2,128,256]{2,1,0:T(8,128)S(1)}, f32[2,128,256]{2,1,0:T(8,128)S(1)}, u32[]{:S(2)}, u32[]{:S(2)}) %collective-permute-start.17) | collective-permute-done | bytes 262176 | tf_op jit(solution)/shard_map/ppermute | solution.py:106
  245.4 14.7 %collective-permute-done.18 = f32[2,128,256]{2,1,0:T(8,128)S(1)} collective-permute-done((f32[2,128,256]{2,1,0:T(8,128)S(1)}, f32[2,128,256]{2,1,0:T(8,128)S(1)}, u32[]{:S(2)}, u32[]{:S(2)}) %collective-permute-start.18) | collective-permute-done | bytes 262176 | tf_op jit(solution)/shard_map/ppermute | solution.py:106
  263.4 40.7 %all_to_all.19 = f32[32,1,128]{2,1,0:T(1,128)} all-to-all(f32[32,1,128]{2,1,0:T(1,128)S(1)} %broadcast_in_dim.7), channel_id=1, replica_groups=mesh['wave'=8,'tile'=32] {'tile'}, dimensions={0} | all-to-all | bytes 32768 | tf_op jit(solution)/shard_map/all_to_all | solution.py:84
  317.7 7.1 %collective-permute-done.22 = f32[256,256]{1,0:T(8,128)} collective-permute-done((f32[256,256]{1,0:T(8,128)}, f32[256,256]{1,0:T(8,128)}, u32[]{:S(2)}, u32[]{:S(2)}) %collective-permute-start.22) | collective-permute-done | bytes 262176 | tf_op jit(solution)/shard_map/ppermute | solution.py:102
  328.0 4.5 fusion.220
  336.8 5.8 %fusion.24 = (f32[2,256,256]{2,1,0:T(8,128)}, f32[2,256,256]{2,1,0:T(8,128)S(1)}) fusion(f32[2,2,512,512]{3,2,1,0:T(8,128)S(1)} %fusion.118, f32[2]{0:T(128)S(1)} %copy-done.9, f32[2]{0:T(128)S(1)} %neg.15, f32[2,256,256]{2,1,0:T(8,128)S(1)} %get-tuple-element.58, f32[2,256,256]{2,1,0:T(8,128)S(1)} %fusion.127, f32[2,256,256]{2,1,0:T(8,128)S(1)} %get-tuple-element.57), kind=kLoop, calls=%fused_computation.37 | loop fusion | flops 7077888 | bytes 6815760 | tf_op jit(solution)/shard_map/reduce_sum | solution.py:76
  345.4 3.6 fusion.12
  350.9 3.4 collective-permute-start.24
  359.0 4.2 collective-permute-done.24
  363.2 11.2 %collective-permute-done.25 = f32[2,256,256]{2,1,0:T(8,128)S(1)} collective-permute-done((f32[2,256,256]{2,1,0:T(8,128)S(1)}, f32[2,256,256]{2,1,0:T(8,128)S(1)}, u32[]{:S(2)}, u32[]{:S(2)}) %collective-permute-start.25) | collective-permute-done | bytes 524320 | tf_op jit(solution)/shard_map/ppermute | solution.py:102
  374.7 3.5 collective-permute-start.26
  379.5 7.5 %collective-permute-done.27 = f32[2,128,256]{2,1,0:T(8,128)S(1)} collective-permute-done((f32[2,128,256]{2,1,0:T(8,128)S(1)}, f32[2,128,256]{2,1,0:T(8,128)S(1)}, u32[]{:S(2)}, u32[]{:S(2)}) %collective-permute-start.27) | collective-permute-done | bytes 262176 | tf_op jit(solution)/shard_map/ppermute | solution.py:106
  387.1 14.7 %collective-permute-done.28 = f32[2,128,256]{2,1,0:T(8,128)S(1)} collective-permute-done((f32[2,128,256]{2,1,0:T(8,128)S(1)}, f32[2,128,256]{2,1,0:T(8,128)S(1)}, u32[]{:S(2)}, u32[]{:S(2)}) %collective-permute-start.28) | collective-permute-done | bytes 262176 | tf_op jit(solution)/shard_map/ppermute | solution.py:106
  405.0 40.6 %all_to_all.20 = f32[32,1,128]{2,1,0:T(1,128)S(1)} all-to-all(f32[32,1,128]{2,1,0:T(1,128)S(1)} %broadcast_in_dim.8), channel_id=1, replica_groups=mesh['wave'=8,'tile'=32] {'tile'}, dimensions={0} | all-to-all | bytes 32768 | tf_op jit(solution)/shard_map/all_to_all | solution.py:84
  (174 shorter events, 129.0 us)
Async XLA Ops:
  0.0 13.9 %collective-permute-start = (f32[256,256]{1,0:T(8,128)}, f32[256,256]{1,0:T(8,128)}, u32[]{:S(2)}, u32[]{:S(2)}) collective-permute-start(f32[256,256]{1,0:T(8,128)} %bitcast.136), channel_id=1, source_target_pairs={{1,0},{33,32},{65,64},{97,96},{129,128},{161,160},{193,192},{225,2... | collective-permute-start | bytes 786440 | tf_op jit(solution)/shard_map/ppermute | solution.py:102
  1.4 12.5 %collective-permute-start.1 = (f32[256,256]{1,0:T(8,128)}, f32[256,256]{1,0:T(8,128)}, u32[]{:S(2)}, u32[]{:S(2)}) collective-permute-start(f32[256,256]{1,0:T(8,128)} %bitcast.137), channel_id=1, source_target_pairs={{8,0},{40,32},{72,64},{104,96},{136,128},{168,160},{200,192},{232,... | collective-permute-start | bytes 786440 | tf_op jit(solution)/shard_map/ppermute | solution.py:102
  2.7 13.7 %collective-permute-start.2 = (f32[256,256]{1,0:T(8,128)}, f32[256,256]{1,0:T(8,128)}, u32[]{:S(2)}, u32[]{:S(2)}) collective-permute-start(f32[256,256]{1,0:T(8,128)} %bitcast.138), channel_id=1, source_target_pairs={{9,0},{41,32},{73,64},{105,96},{137,128},{169,160},{201,192},{233,... | collective-permute-start | bytes 786440 | tf_op jit(solution)/shard_map/ppermute | solution.py:102
  46.8 15.3 %collective-permute-start.3 = (f32[2,256,256]{2,1,0:T(8,128)}, f32[2,256,256]{2,1,0:T(8,128)S(1)}, u32[]{:S(2)}, u32[]{:S(2)}) collective-permute-start(f32[2,256,256]{2,1,0:T(8,128)} %get-tuple-element.48), channel_id=1, source_target_pairs={{0,1},{32,33},{64,65},{96,97},{128,129},{160,161},{192,193},{224,2... | collective-permute-start | bytes 1572872 | tf_op jit(solution)/shard_map/ppermute | solution.py:102
  52.4 12.6 %collective-permute-start.4 = (f32[2,256,256]{2,1,0:T(8,128)}, f32[2,256,256]{2,1,0:T(8,128)}, u32[]{:S(2)}, u32[]{:S(2)}) collective-permute-start(f32[2,256,256]{2,1,0:T(8,128)} %get-tuple-element.50), channel_id=1, source_target_pairs={{0,8},{32,40},{64,72},{96,104},{128,136},{160,168},{192,200},{224,... | collective-permute-start | bytes 1572872 | tf_op jit(solution)/shard_map/ppermute | solution.py:102
  56.3 19.9 %collective-permute-start.5 = (f32[2,256,256]{2,1,0:T(8,128)}, f32[2,256,256]{2,1,0:T(8,128)}, u32[]{:S(2)}, u32[]{:S(2)}) collective-permute-start(f32[2,256,256]{2,1,0:T(8,128)} %get-tuple-element.49), channel_id=1, source_target_pairs={{0,9},{32,41},{64,73},{96,105},{128,137},{160,169},{192,201},{224,... | collective-permute-start | bytes 1572872 | tf_op jit(solution)/shard_map/ppermute | solution.py:102
  78.6 4.8 %collective-permute-start.6 = (f32[2,128,256]{2,1,0:T(8,128)}, f32[2,128,256]{2,1,0:T(8,128)}, u32[]{:S(2)}, u32[]{:S(2)}) collective-permute-start(f32[2,128,256]{2,1,0:T(8,128)} %constant_dynamic-slice_fusion.2), channel_id=1, source_target_pairs={{0,32},{32,0},{64,96},{96,64},{128,160},{160,128},{192,224},{224,1... | collective-permute-start | bytes 786440 | tf_op jit(solution)/shard_map/ppermute | solution.py:106
  84.4 82.2 %copy-start.16 = (s32[2]{0:T(128)S(1)}, s32[2]{0:T(128)}, u32[]{:S(2)}) copy-start(s32[2]{0:T(128)} %get-tuple-element.69) | copy-start | bytes 28
  84.4 7.9 %collective-permute-start.7 = (f32[2,128,256]{2,1,0:T(8,128)S(1)}, f32[2,128,256]{2,1,0:T(8,128)S(1)}, u32[]{:S(2)}, u32[]{:S(2)}) collective-permute-start(f32[2,128,256]{2,1,0:T(8,128)S(1)} %dynamic-slice_add_fusion.2), channel_id=1, source_target_pairs={{0,64},{32,96},{64,0},{96,32},{128,192},{160,224},{192,128},{224,1... | collective-permute-start | bytes 786440 | tf_op jit(solution)/shard_map/ppermute | solution.py:106
  92.4 14.4 %collective-permute-start.8 = (f32[2,128,256]{2,1,0:T(8,128)S(1)}, f32[2,128,256]{2,1,0:T(8,128)S(1)}, u32[]{:S(2)}, u32[]{:S(2)}) collective-permute-start(f32[2,128,256]{2,1,0:T(8,128)S(1)} %add.337), channel_id=1, source_target_pairs={{0,128},{32,160},{64,192},{96,224},{128,0},{160,32},{192,64},{224,... | collective-permute-start | bytes 786440 | tf_op jit(solution)/shard_map/ppermute | solution.py:106
  106.9 2.9 collective-permute-start.9
  162.7 8.4 %collective-permute-start.10 = (f32[256,256]{1,0:T(8,128)}, f32[256,256]{1,0:T(8,128)}, u32[]{:S(2)}, u32[]{:S(2)}) collective-permute-start(f32[256,256]{1,0:T(8,128)} %get-tuple-element.22), channel_id=1, source_target_pairs={{1,0},{33,32},{65,64},{97,96},{129,128},{161,160},{193,192},{225,2... | collective-permute-start | bytes 786440 | tf_op jit(solution)/shard_map/ppermute | solution.py:102
  164.0 8.4 %collective-permute-start.11 = (f32[256,256]{1,0:T(8,128)}, f32[256,256]{1,0:T(8,128)}, u32[]{:S(2)}, u32[]{:S(2)}) collective-permute-start(f32[256,256]{1,0:T(8,128)} %get-tuple-element.22), channel_id=1, source_target_pairs={{8,0},{40,32},{72,64},{104,96},{136,128},{168,160},{200,192},{232,... | collective-permute-start | bytes 786440 | tf_op jit(solution)/shard_map/ppermute | solution.py:102
  165.3 14.3 %collective-permute-start.12 = (f32[256,256]{1,0:T(8,128)}, f32[256,256]{1,0:T(8,128)}, u32[]{:S(2)}, u32[]{:S(2)}) collective-permute-start(f32[256,256]{1,0:T(8,128)} %get-tuple-element.22), channel_id=1, source_target_pairs={{9,0},{41,32},{73,64},{105,96},{137,128},{169,160},{201,192},{233,... | collective-permute-start | bytes 786440 | tf_op jit(solution)/shard_map/ppermute | solution.py:102
  207.5 9.9 %collective-permute-start.13 = (f32[2,256,256]{2,1,0:T(8,128)S(1)}, f32[2,256,256]{2,1,0:T(8,128)S(1)}, u32[]{:S(2)}, u32[]{:S(2)}) collective-permute-start(f32[2,256,256]{2,1,0:T(8,128)S(1)} %get-tuple-element.45), channel_id=1, source_target_pairs={{0,1},{32,33},{64,65},{96,97},{128,129},{160,161},{192,193},{224,2... | collective-permute-start | bytes 1572872 | tf_op jit(solution)/shard_map/ppermute | solution.py:102
  209.3 12.3 %collective-permute-start.14 = (f32[2,256,256]{2,1,0:T(8,128)S(1)}, f32[2,256,256]{2,1,0:T(8,128)S(1)}, u32[]{:S(2)}, u32[]{:S(2)}) collective-permute-start(f32[2,256,256]{2,1,0:T(8,128)S(1)} %get-tuple-element.47), channel_id=1, source_target_pairs={{0,8},{32,40},{64,72},{96,104},{128,136},{160,168},{192,200},{224,... | collective-permute-start | bytes 1572872 | tf_op jit(solution)/shard_map/ppermute | solution.py:102
  212.7 20.1 %collective-permute-start.15 = (f32[2,256,256]{2,1,0:T(8,128)S(1)}, f32[2,256,256]{2,1,0:T(8,128)S(1)}, u32[]{:S(2)}, u32[]{:S(2)}) collective-permute-start(f32[2,256,256]{2,1,0:T(8,128)S(1)} %get-tuple-element.46), channel_id=1, source_target_pairs={{0,9},{32,41},{64,73},{96,105},{128,137},{160,169},{192,201},{224,... | collective-permute-start | bytes 1572872 | tf_op jit(solution)/shard_map/ppermute | solution.py:102
  233.0 4.7 %collective-permute-start.16 = (f32[2,128,256]{2,1,0:T(8,128)S(1)}, f32[2,128,256]{2,1,0:T(8,128)S(1)}, u32[]{:S(2)}, u32[]{:S(2)}) collective-permute-start(f32[2,128,256]{2,1,0:T(8,128)S(1)} %constant_dynamic-slice_fusion.1), channel_id=1, source_target_pairs={{0,32},{32,0},{64,96},{96,64},{128,160},{160,128},{192,224},{224,1... | collective-permute-start | bytes 786440 | tf_op jit(solution)/shard_map/ppermute | solution.py:106
  237.7 7.6 %collective-permute-start.17 = (f32[2,128,256]{2,1,0:T(8,128)S(1)}, f32[2,128,256]{2,1,0:T(8,128)S(1)}, u32[]{:S(2)}, u32[]{:S(2)}) collective-permute-start(f32[2,128,256]{2,1,0:T(8,128)S(1)} %dynamic-slice_add_fusion.1), channel_id=1, source_target_pairs={{0,64},{32,96},{64,0},{96,32},{128,192},{160,224},{192,128},{224,1... | collective-permute-start | bytes 786440 | tf_op jit(solution)/shard_map/ppermute | solution.py:106
  245.3 14.8 %collective-permute-start.18 = (f32[2,128,256]{2,1,0:T(8,128)S(1)}, f32[2,128,256]{2,1,0:T(8,128)S(1)}, u32[]{:S(2)}, u32[]{:S(2)}) collective-permute-start(f32[2,128,256]{2,1,0:T(8,128)S(1)} %add.364), channel_id=1, source_target_pairs={{0,128},{32,160},{64,192},{96,224},{128,0},{160,32},{192,64},{224,... | collective-permute-start | bytes 786440 | tf_op jit(solution)/shard_map/ppermute | solution.py:106
  260.2 1.7 collective-permute-start.19
  308.0 8.4 %collective-permute-start.20 = (f32[256,256]{1,0:T(8,128)}, f32[256,256]{1,0:T(8,128)}, u32[]{:S(2)}, u32[]{:S(2)}) collective-permute-start(f32[256,256]{1,0:T(8,128)} %get-tuple-element.20), channel_id=1, source_target_pairs={{1,0},{33,32},{65,64},{97,96},{129,128},{161,160},{193,192},{225,2... | collective-permute-start | bytes 786440 | tf_op jit(solution)/shard_map/ppermute | solution.py:102
  309.3 8.4 %collective-permute-start.21 = (f32[256,256]{1,0:T(8,128)}, f32[256,256]{1,0:T(8,128)}, u32[]{:S(2)}, u32[]{:S(2)}) collective-permute-start(f32[256,256]{1,0:T(8,128)} %get-tuple-element.20), channel_id=1, source_target_pairs={{8,0},{40,32},{72,64},{104,96},{136,128},{168,160},{200,192},{232,... | collective-permute-start | bytes 786440 | tf_op jit(solution)/shard_map/ppermute | solution.py:102
  310.6 14.3 %collective-permute-start.22 = (f32[256,256]{1,0:T(8,128)}, f32[256,256]{1,0:T(8,128)}, u32[]{:S(2)}, u32[]{:S(2)}) collective-permute-start(f32[256,256]{1,0:T(8,128)} %get-tuple-element.20), channel_id=1, source_target_pairs={{9,0},{41,32},{73,64},{105,96},{137,128},{169,160},{201,192},{233,... | collective-permute-start | bytes 786440 | tf_op jit(solution)/shard_map/ppermute | solution.py:102
  349.1 9.9 %collective-permute-start.23 = (f32[2,256,256]{2,1,0:T(8,128)S(1)}, f32[2,256,256]{2,1,0:T(8,128)S(1)}, u32[]{:S(2)}, u32[]{:S(2)}) collective-permute-start(f32[2,256,256]{2,1,0:T(8,128)S(1)} %get-tuple-element.42), channel_id=1, source_target_pairs={{0,1},{32,33},{64,65},{96,97},{128,129},{160,161},{192,193},{224,2... | collective-permute-start | bytes 1572872 | tf_op jit(solution)/shard_map/ppermute | solution.py:102
  350.9 12.3 %collective-permute-start.24 = (f32[2,256,256]{2,1,0:T(8,128)S(1)}, f32[2,256,256]{2,1,0:T(8,128)S(1)}, u32[]{:S(2)}, u32[]{:S(2)}) collective-permute-start(f32[2,256,256]{2,1,0:T(8,128)S(1)} %get-tuple-element.44), channel_id=1, source_target_pairs={{0,8},{32,40},{64,72},{96,104},{128,136},{160,168},{192,200},{224,... | collective-permute-start | bytes 1572872 | tf_op jit(solution)/shard_map/ppermute | solution.py:102
  354.4 20.1 %collective-permute-start.25 = (f32[2,256,256]{2,1,0:T(8,128)S(1)}, f32[2,256,256]{2,1,0:T(8,128)S(1)}, u32[]{:S(2)}, u32[]{:S(2)}) collective-permute-start(f32[2,256,256]{2,1,0:T(8,128)S(1)} %get-tuple-element.43), channel_id=1, source_target_pairs={{0,9},{32,41},{64,73},{96,105},{128,137},{160,169},{192,201},{224,... | collective-permute-start | bytes 1572872 | tf_op jit(solution)/shard_map/ppermute | solution.py:102
  374.6 72.2 %copy-start.4 = (f32[1,256,256]{2,1,0:T(8,128)S(1)}, f32[1,256,256]{2,1,0:T(8,128)}, u32[]{:S(2)}) copy-start(f32[1,256,256]{2,1,0:T(8,128)} %param.8) | copy-start | bytes 786436
  374.7 4.7 %collective-permute-start.26 = (f32[2,128,256]{2,1,0:T(8,128)S(1)}, f32[2,128,256]{2,1,0:T(8,128)S(1)}, u32[]{:S(2)}, u32[]{:S(2)}) collective-permute-start(f32[2,128,256]{2,1,0:T(8,128)S(1)} %constant_dynamic-slice_fusion), channel_id=1, source_target_pairs={{0,32},{32,0},{64,96},{96,64},{128,160},{160,128},{192,224},{224,1... | collective-permute-start | bytes 786440 | tf_op jit(solution)/shard_map/ppermute | solution.py:106
  379.4 7.6 %collective-permute-start.27 = (f32[2,128,256]{2,1,0:T(8,128)S(1)}, f32[2,128,256]{2,1,0:T(8,128)S(1)}, u32[]{:S(2)}, u32[]{:S(2)}) collective-permute-start(f32[2,128,256]{2,1,0:T(8,128)S(1)} %dynamic-slice_add_fusion), channel_id=1, source_target_pairs={{0,64},{32,96},{64,0},{96,32},{128,192},{160,224},{192,128},{224,1... | collective-permute-start | bytes 786440 | tf_op jit(solution)/shard_map/ppermute | solution.py:106
  387.0 14.8 %collective-permute-start.28 = (f32[2,128,256]{2,1,0:T(8,128)S(1)}, f32[2,128,256]{2,1,0:T(8,128)S(1)}, u32[]{:S(2)}, u32[]{:S(2)}) collective-permute-start(f32[2,128,256]{2,1,0:T(8,128)S(1)} %add.391), channel_id=1, source_target_pairs={{0,128},{32,160},{64,192},{96,224},{128,0},{160,32},{192,64},{224,... | collective-permute-start | bytes 786440 | tf_op jit(solution)/shard_map/ppermute | solution.py:106
  401.9 1.7 collective-permute-start.29
  (18 other events, 224.5 us)
